TPU v7x, 128 devices: a whole 4x4x4 slice. The times are simulated.
128 devices in a mesh: expert: 16 (over y, x_lo, core), tensor: 8 (over x_hi, z).
Axes of the slice: x: 4 (x_hi: 2, x_lo: 2; x = x_hi * 2 + x_lo), y: 4, z: 4, core: 2. Of those that a mesh axis runs over, the one named last changes fastest.
Arguments:
- slot_choices: int32 [4096, 4], P('expert'), may hold values from 0 to 31, all different within a row; in each aligned block of 256 rows (0 to 255, 256 to 511, ...) at most 40 rows name the same one
- mix_weights: float32 [4096, 4], P('expert'), may hold values from 0.1 to 2.5
- tokens: bfloat16 [4096, 3584], P('expert'), may hold values from -6 to 6
- cotangent: bfloat16 [4096, 3584], P('expert'), may hold values from -0.71875 to 0.71875
- hot_experts: int32 [2], replicated, may hold values from 0 to 15, as said below
- replica_of: int32 [16], replicated, may hold values from 0 to 15, as said below
- weights_in: bfloat16 [16, 2, 3584, 1024], P('expert', None, None, 'tensor'), may hold values from -0.1796875 to 0.1796875
- weights_down: bfloat16 [16, 1024, 3584], P('expert', 'tensor'), may hold values from -0.1796875 to 0.1796875
- mean_in: bfloat16 [16, 2, 3584, 1024], P('expert', None, None, 'tensor'), may hold values from -1.796875 to 1.796875
- mean_down: bfloat16 [16, 1024, 3584], P('expert', 'tensor'), may hold values from -1.796875 to 1.796875
- square_in: bfloat16 [16, 2, 3584, 1024], P('expert', None, None, 'tensor'), may hold values from 0.099609375 to 1
- square_down: bfloat16 [16, 1024, 3584], P('expert', 'tensor'), may hold values from 0.099609375 to 1
Outputs:
- stepped_in: bfloat16 [16, 2, 3584, 1024], P('expert', None, None, 'tensor')
- stepped_down: bfloat16 [16, 1024, 3584], P('expert', 'tensor')
- averaged_in: bfloat16 [16, 2, 3584, 1024], P('expert', None, None, 'tensor')
- averaged_down: bfloat16 [16, 1024, 3584], P('expert', 'tensor')
- squared_in: bfloat16 [16, 2, 3584, 1024], P('expert', None, None, 'tensor')
- squared_down: bfloat16 [16, 1024, 3584], P('expert', 'tensor')
- copied_in: bfloat16 [16, 2, 3584, 1024], P('expert', None, None, 'tensor')
- copied_down: bfloat16 [16, 1024, 3584], P('expert', 'tensor')
Inputs may be any that keep to these rules, and one draw needn't show every extreme that they name: `slot_choices`: within the 256 tokens of one index of expert, no slot is named by more than 40 choices; the 4 slots of one token differ. `hot_experts`: 2 different experts, one of them expert 16 - 1. `replica_of`: entry j is one of hot_experts and never j; each of hot_experts is named by some entry.
All inputs are finite; a program needn't handle non-finite values.
Results may differ from a plain program's by a relative error of at most 0.023.
Values may be sent and summed in bfloat16 or wider, within the bound.
No kernel may reach another device: no remote copies, remote signals or barrier semaphores. Data moves between devices by JAX's collectives and lax.ppermute only.
A program may use at most 192 MiB of HBM per device.

v0:
```python
import math

import jax
import jax.numpy as jnp
from jax import lax
from jax.sharding import PartitionSpec as P

beta_one = 0.9
beta_two = 0.95
learn_rate = 0.02
decay_rate = 0.1
epsilon = 1e-08
weight_scale = 0.03


def broadcast(block, axis, source):
    block = jnp.where(lax.axis_index(axis) == source, block, jnp.zeros_like(block))
    return lax.psum(block, axis)


def adam_step(weight, moment_one, moment_two, gradient):
    first_new = beta_one * moment_one.astype(jnp.float32) + (1.0 - beta_one) * gradient
    second_new = beta_two * moment_two.astype(jnp.float32) + (1.0 - beta_two) * gradient * gradient
    base_val = weight.astype(jnp.float32)
    weight_new = base_val - learn_rate * (
        first_new / (jnp.sqrt(second_new) + epsilon) + decay_rate * base_val
    )
    return (
        weight_new.astype(jnp.bfloat16),
        first_new.astype(jnp.bfloat16),
        second_new.astype(jnp.bfloat16),
    )


def route_rows(slot_choices, mix_weights, slot_count, capacity, row_count):
    top_count = slot_choices.shape[1]
    flat_ids = slot_choices.reshape(-1)
    entries = flat_ids.shape[0]
    onehot = (flat_ids[:, None] == jnp.arange(slot_count, dtype=jnp.int32)[None, :]).astype(
        jnp.int32
    )
    before = jnp.cumsum(onehot, axis=0) - onehot
    position = jnp.sum(before * onehot, axis=1)
    target = flat_ids * capacity + position
    wanted = (
        jnp.arange(slot_count, dtype=jnp.int32)[:, None] * capacity
        + jnp.arange(row_count, dtype=jnp.int32)[None, :]
    ).reshape(-1)
    matches = wanted[:, None] == target[None, :]
    present = jnp.any(matches, axis=1)
    source = jnp.sum(jnp.where(matches, jnp.arange(entries, dtype=jnp.int32)[None, :], 0), axis=1)
    weight = jnp.where(present, mix_weights.reshape(-1)[source], 0.0)
    return source // top_count, present, weight


def gather_rows(token_index, present, weight, tokens, cotangent, slot_count, row_count):
    rows_token = jnp.where(present[:, None], tokens[token_index], jnp.zeros((), tokens.dtype))
    rows_cotan = (weight[:, None] * cotangent[token_index].astype(jnp.float32)).astype(jnp.bfloat16)
    row_shape = (slot_count // 2, 2, row_count, tokens.shape[1])
    return (rows_token.reshape(row_shape), rows_cotan.reshape(row_shape))


def slot_terms(rows_token, rows_cotan, weight_in, weight_down, scale_in, scale_down):
    joined = (
        jnp.einsum("rd,gdf->grf", rows_token, weight_in, preferred_element_type=jnp.float32)
        * scale_in
    )
    gate_val = joined[0]
    up_val = joined[1]
    sigmoid_val = jax.nn.sigmoid(gate_val)
    active = gate_val * sigmoid_val
    hidden = (active * up_val).astype(jnp.bfloat16)
    back_grad = (
        jnp.einsum("rd,fd->rf", rows_cotan, weight_down, preferred_element_type=jnp.float32)
        * scale_down
    )
    slope_gate = (back_grad * up_val * sigmoid_val * (1.0 + gate_val * (1.0 - sigmoid_val))).astype(
        jnp.bfloat16
    )
    slope_up = (back_grad * active).astype(jnp.bfloat16)
    slopes = jnp.stack([slope_gate, slope_up])
    grad_in = jnp.einsum("rd,grf->gdf", rows_token, slopes, preferred_element_type=jnp.float32)
    grad_down = jnp.einsum("rf,rd->fd", hidden, rows_cotan, preferred_element_type=jnp.float32)
    return (grad_in, grad_down)


def pack(part_in, part_down, groups):
    width = part_in.shape[1]
    inner = part_in.shape[2]
    return jnp.concatenate(
        [
            part_in.reshape(groups, 2 * width // groups, inner),
            part_down.reshape(groups, width // groups, inner),
        ],
        axis=1,
    )


def unpack(packed, width, inner):
    groups = packed.shape[0]
    split = 2 * width // groups
    part_in = packed[:, :split].reshape(2, width, inner)
    part_down = packed[:, split:].reshape(inner, width)
    return part_in, part_down


def exchange(block):
    return lax.all_to_all(block, "expert", 0, 0, tiled=True)


def spread_chosen(arrived, hot_experts, replica_of):
    first = lax.dynamic_index_in_dim(arrived, hot_experts[0], 0, keepdims=False)
    second = lax.dynamic_index_in_dim(arrived, hot_experts[1], 0, keepdims=False)
    wants_first = (replica_of == hot_experts[0])[:, None, None]
    outgoing = jnp.where(wants_first, first[None], second[None])
    return exchange(outgoing)


def spread_hot(packed, hot_experts, replica_of):
    return spread_chosen(exchange(packed), hot_experts, replica_of)


def body(
    slot_choices,
    mix_weights,
    tokens,
    cotangent,
    hot_experts,
    replica_of,
    weights_in,
    weights_down,
    mean_in,
    mean_down,
    square_in,
    square_down,
):
    expert_count = lax.axis_size("expert")
    tensor_count = lax.axis_size("tensor")
    token_count = slot_choices.shape[0]
    top_count = slot_choices.shape[1]
    share = (5 * token_count * top_count + 8 * expert_count * tensor_count - 1) // (
        8 * expert_count * tensor_count
    )
    capacity = share * tensor_count
    own_index = lax.axis_index("expert")
    own_in = weights_in[0]
    own_down = weights_down[0]
    width = tokens.shape[1]
    inner = own_in.shape[2]
    scale_in = 1.0 / (weight_scale * math.sqrt(width))
    scale_down = 1.0 / (weight_scale * math.sqrt(inner * tensor_count))
    own_packed = pack(own_in, own_down, expert_count)
    first_arrived = exchange(own_packed)
    token_index, present, row_weight = route_rows(
        slot_choices, mix_weights, 2 * expert_count, capacity, capacity
    )
    first_arrived, token_index, present, row_weight = lax.optimization_barrier(
        (first_arrived, token_index, present, row_weight)
    )
    held_in, held_down = unpack(
        spread_chosen(first_arrived, hot_experts, replica_of), width, inner
    )
    weight_sets = ((own_in, own_down), (held_in, held_down))
    built_token, built_cotan = gather_rows(
        token_index, present, row_weight, tokens, cotangent, 2 * expert_count, capacity
    )

    def rows_of(add_which):
        outgoing = jnp.stack([built_token[:, add_which], built_cotan[:, add_which]], axis=1)
        return exchange(outgoing)

    def terms_of(arrived_rows, add_which):
        return slot_terms(
            arrived_rows[:, 0].reshape(-1, width),
            arrived_rows[:, 1].reshape(-1, width),
            weight_sets[add_which][0],
            weight_sets[add_which][1],
            scale_in,
            scale_down,
        )

    copy_rows = rows_of(1)
    copy_in, copy_down = terms_of(copy_rows, 1)
    own_rows = rows_of(0)
    copy_packed = pack(
        (copy_in * scale_in).astype(jnp.bfloat16),
        (copy_down * scale_down).astype(jnp.bfloat16),
        expert_count,
    )
    copy_packed, own_rows = lax.optimization_barrier((copy_packed, own_rows))
    grad_in, grad_down = terms_of(own_rows, 0)
    grad_in = grad_in * scale_in
    grad_down = grad_down * scale_down
    arrived = exchange(copy_packed).astype(jnp.float32)
    sources = jnp.arange(expert_count, dtype=jnp.int32)
    sums = []
    for which in range(2):
        picked = (replica_of == hot_experts[which])[:, None, None]
        sums.append(jnp.sum(jnp.where(picked, arrived, 0.0), axis=0))
    to_owner = jnp.where(
        (sources == hot_experts[0])[:, None, None],
        sums[0][None],
        jnp.where((sources == hot_experts[1])[:, None, None], sums[1][None], 0.0),
    ).astype(jnp.bfloat16)
    gathered = exchange(to_owner).astype(jnp.float32)
    is_hot = jnp.any(hot_experts == own_index)
    own_grad = pack(grad_in, grad_down, expert_count)
    total = jnp.where(is_hot, own_grad.astype(jnp.bfloat16).astype(jnp.float32) + gathered, own_grad)
    stepped_p, averaged_p, squared_p = adam_step(
        own_packed,
        pack(mean_in[0], mean_down[0], expert_count),
        pack(square_in[0], square_down[0], expert_count),
        total,
    )
    copied_in, copied_down = unpack(spread_hot(stepped_p, hot_experts, replica_of), width, inner)
    stepped_in, stepped_down = unpack(stepped_p, width, inner)
    averaged_in, averaged_down = unpack(averaged_p, width, inner)
    squared_in, squared_down = unpack(squared_p, width, inner)
    return (
        stepped_in[None],
        stepped_down[None],
        averaged_in[None],
        averaged_down[None],
        squared_in[None],
        squared_down[None],
        copied_in[None],
        copied_down[None],
    )


def solution(mesh):
    placed = (
        P("expert", None),
        P("expert", None),
        P("expert", None),
        P("expert", None),
        P(),
        P(),
        P("expert", None, None, "tensor"),
        P("expert", "tensor", None),
        P("expert", None, None, "tensor"),
        P("expert", "tensor", None),
        P("expert", None, None, "tensor"),
        P("expert", "tensor", None),
    )
    return jax.shard_map(
        body,
        mesh=mesh,
        in_specs=placed,
        out_specs=(
            P("expert", None, None, "tensor"),
            P("expert", "tensor", None),
            P("expert", None, None, "tensor"),
            P("expert", "tensor", None),
            P("expert", None, None, "tensor"),
            P("expert", "tensor", None),
            P("expert", None, None, "tensor"),
            P("expert", "tensor", None),
        ),
        check_vma=False,
    )
```

profile of v0, /device:TPU:1, one launch (start us, length us, event | category | flops | bytes accessed | tf_op | source)
XLA Modules:
  0.0 522.2 jit_solution(4789536477683400673)
XLA Ops:
  0.6 2.4 reshape_squeeze.31
  3.1 3.6 pad_maximum_fusion.3
  6.7 7.0 %all-to-all-start = ((bf16[16,672,128]{2,1,0:T(8,128)(2,1)}), bf16[16,672,128]{2,1,0:T(8,128)(2,1)}, u32[]{:S(2)}, u32[]{:S(2)}) async-start(bf16[16,672,128]{2,1,0:T(8,128)(2,1)} %pad_maximum_fusion.3), calls=%async_computation | async-start | bytes 5505024 | tf_op jit(solution)/shard_map/all_to_all | solution.py:108
  17.3 9.0 %reduce-window.6 = s32[32,8,128]{2,1,0:T(8,128)S(1)} reduce-window(s32[32,8,128]{2,1,0:T(8,128)S(1)} %fusion.58, s32[]{:T(128)} %constant.29.clone.1), window={size=1x1x128 pad=0_0x0_0x127_0}, to_apply=%region_1.2 | reduce-window | flops 4161536 | bytes 262148 | tf_op jit(solution)/shard_map/reduce-window
  28.2 5.0 gather_fusion
  36.6 11.2 %all-to-all-done = bf16[16,672,128]{2,1,0:T(8,128)(2,1)} async-done(((bf16[16,672,128]{2,1,0:T(8,128)(2,1)}), bf16[16,672,128]{2,1,0:T(8,128)(2,1)}, u32[]{:S(2)}, u32[]{:S(2)}) %all-to-all-start) | async-done | bytes 2752544 | tf_op jit(solution)/shard_map/all_to_all | solution.py:108
  47.9 7.8 %gather_fusion.2 = bf16[1280,3584]{1,0:T(8,128)(2,1)} fusion(bf16[256,3584]{1,0:T(8,128)(2,1)S(1)} %copy-done, s32[2048]{0:T(1024)S(1)} %pad_clamp_fusion), kind=kCustom, calls=%fused_computation.2 | custom fusion | bytes 18355200 | tf_op jit(solution)/shard_map/gather | solution.py:58
  55.7 18.8 %gather_fusion.1 = bf16[1280,3584]{1,0:T(8,128)(2,1)} fusion(bf16[256,3584]{1,0:T(8,128)(2,1)} %param.14, s32[2048]{0:T(1024)S(1)} %pad_clamp_fusion), kind=kCustom, calls=%fused_computation.1 | custom fusion | bytes 18355200 | tf_op jit(solution)/shard_map/gather | solution.py:57
  77.6 5.5 %all-to-all-start.2 = ((bf16[16,672,128]{2,1,0:T(8,128)(2,1)}), bf16[16,672,128]{2,1,0:T(8,128)(2,1)}, u32[]{:S(2)}, u32[]{:S(2)}) async-start(bf16[16,672,128]{2,1,0:T(8,128)(2,1)} %broadcast_select_fusion.2), calls=%async_computation.2 | async-start | bytes 5505024 | tf_op jit(solution)/shard_map/all_to_all | solution.py:108
  83.1 10.6 %fusion = bf16[16,2,40,3584]{3,2,1,0:T(8,128)(2,1)} fusion(bf16[16,2,40,3584]{3,2,1,0:T(8,128)(2,1)} %bitcast.166, f32[16,2,40]{2,1,0:T(2,128)S(1)} %mul.159), kind=kLoop, calls=%fused_computation.4 | loop fusion | flops 13762560 | bytes 18355200 | tf_op jit(solution)/shard_map/convert_element_type | solution.py:58
  93.6 7.9 %broadcast_select_fusion = bf16[16,2,40,3584]{3,2,1,0:T(8,128)(2,1)} fusion(bf16[16,2,40,3584]{3,2,1,0:T(8,128)(2,1)} %bitcast.165, pred[16,2,40]{2,1,0:T(4,128)(4,1)S(1)} %broadcast_in_dim.152), kind=kLoop, calls=%fused_computation.7 | loop fusion | flops 4587520 | bytes 18351360 | tf_op jit(solution)/shard_map/jit(_where)/select_n | solution.py:57
  101.6 13.2 %fusion.67 = (bf16[16,1,40,3584]{3,2,1,0:T(8,128)(2,1)}, bf16[16,1,40,3584]{3,2,1,0:T(8,128)(2,1)}, bf16[16,1,40,3584]{3,2,1,0:T(8,128)(2,1)}, bf16[16,1,40,3584]{3,2,1,0:T(8,128)(2,1)}) fusion(bf16[16,2,40,3584]{3,2,1,0:T(8,128)(2,1)} %broadcast_select_fusion, bf16[16,2,40,3584]{3,2,1,0:T(8,128)(2,1)} %fusion), kind=kLoop, calls=%fused_computation.130 | loop fusion | bytes 36700160 | tf_op jit(solution)/shard_map/slice | solution.py:169
  114.8 8.1 %pad_maximum_fusion = bf16[16,2,40,3584]{3,2,1,0:T(8,128)(2,1)} fusion(bf16[16,1,40,3584]{3,2,1,0:T(8,128)(2,1)} %get-tuple-element.45, bf16[16,1,40,3584]{3,2,1,0:T(8,128)(2,1)} %get-tuple-element.28), kind=kLoop, calls=%fused_computation.5 | loop fusion | flops 4587520 | bytes 18350080 | tf_op jit(solution)/shard_map/stack | solution.py:169
  122.9 5.8 %all-to-all-start.1 = ((bf16[16,2,40,3584]{3,2,1,0:T(8,128)(2,1)}), bf16[16,2,40,3584]{3,2,1,0:T(8,128)(2,1)}, u32[]{:S(2)}, u32[]{:S(2)}) async-start(bf16[16,2,40,3584]{3,2,1,0:T(8,128)(2,1)} %pad_maximum_fusion), calls=%async_computation.1 | async-start | bytes 18350080 | tf_op jit(solution)/shard_map/all_to_all | solution.py:108
  128.7 8.1 %pad_maximum_fusion.1 = bf16[16,2,40,3584]{3,2,1,0:T(8,128)(2,1)} fusion(bf16[16,1,40,3584]{3,2,1,0:T(8,128)(2,1)} %get-tuple-element.46, bf16[16,1,40,3584]{3,2,1,0:T(8,128)(2,1)} %get-tuple-element.27), kind=kLoop, calls=%fused_computation.6 | loop fusion | flops 4587520 | bytes 18350080 | tf_op jit(solution)/shard_map/stack | solution.py:169
  136.8 94.8 %all-to-all-done.1 = bf16[16,2,40,3584]{3,2,1,0:T(8,128)(2,1)} async-done(((bf16[16,2,40,3584]{3,2,1,0:T(8,128)(2,1)}), bf16[16,2,40,3584]{3,2,1,0:T(8,128)(2,1)}, u32[]{:S(2)}, u32[]{:S(2)}) %all-to-all-start.1) | async-done | bytes 9175072 | tf_op jit(solution)/shard_map/all_to_all | solution.py:108
  231.5 5.8 %all-to-all-start.3 = ((bf16[16,2,40,3584]{3,2,1,0:T(8,128)(2,1)}), bf16[16,2,40,3584]{3,2,1,0:T(8,128)(2,1)}, u32[]{:S(2)}, u32[]{:S(2)}) async-start(bf16[16,2,40,3584]{3,2,1,0:T(8,128)(2,1)} %pad_maximum_fusion.1), calls=%async_computation.3 | async-start | bytes 18350080 | tf_op jit(solution)/shard_map/all_to_all | solution.py:108
  238.6 1.9 reshape.132
  242.2 4.3 fusion.69
  250.0 2.9 fusion.10
  252.9 2.9 copy.59
  255.8 3.2 fusion.11
  259.1 2.1 reshape.135
  261.2 2.9 pad_maximum_fusion.5
  264.1 76.1 %all-to-all-done.3 = bf16[16,2,40,3584]{3,2,1,0:T(8,128)(2,1)} async-done(((bf16[16,2,40,3584]{3,2,1,0:T(8,128)(2,1)}), bf16[16,2,40,3584]{3,2,1,0:T(8,128)(2,1)}, u32[]{:S(2)}, u32[]{:S(2)}) %all-to-all-start.3) | async-done | bytes 9175072 | tf_op jit(solution)/shard_map/all_to_all | solution.py:108
  340.2 5.2 all-to-all-start.4
  345.4 2.1 reshape_squeeze.33
  347.5 2.1 reshape_squeeze.39
  351.5 28.1 %all-to-all-done.4 = bf16[16,672,128]{2,1,0:T(8,128)(2,1)} async-done(((bf16[16,672,128]{2,1,0:T(8,128)(2,1)}), bf16[16,672,128]{2,1,0:T(8,128)(2,1)}, u32[]{:S(2)}, u32[]{:S(2)}) %all-to-all-start.4) | async-done | bytes 2752544 | tf_op jit(solution)/shard_map/all_to_all | solution.py:108
  379.6 3.0 fusion.4
  382.5 2.3 select_convert_fusion
  384.9 5.4 %all-to-all-start.5 = ((bf16[16,672,128]{2,1,0:T(8,128)(2,1)}), bf16[16,672,128]{2,1,0:T(8,128)(2,1)}, u32[]{:S(2)}, u32[]{:S(2)}) async-start(bf16[16,672,128]{2,1,0:T(8,128)(2,1)} %select_convert_fusion), calls=%async_computation.5 | async-start | bytes 5505024 | tf_op jit(solution)/shard_map/all_to_all | solution.py:108
  390.3 4.4 fusion.66
  398.2 3.5 fusion.7
  401.6 5.2 %copy.61 = f32[2,3584,128]{2,1,0:T(8,128)} copy(f32[2,3584,128]{1,2,0:T(8,128)} %fusion.7) | data formatting | bytes 7340032 | tf_op jit(solution)/shard_map/mul | solution.py:192
  406.9 4.6 convolution_multiply_fusion.2
  411.5 2.6 reshape.137
  414.1 10.4 %all-to-all-done.5 = bf16[16,672,128]{2,1,0:T(8,128)(2,1)} async-done(((bf16[16,672,128]{2,1,0:T(8,128)(2,1)}), bf16[16,672,128]{2,1,0:T(8,128)(2,1)}, u32[]{:S(2)}, u32[]{:S(2)}) %all-to-all-start.5) | async-done | bytes 2752544 | tf_op jit(solution)/shard_map/all_to_all | solution.py:108
  424.5 10.5 %fusion.14 = (bf16[16,672,128]{2,1,0:T(8,128)(2,1)}, bf16[16,672,128]{2,1,0:T(8,128)(2,1)S(1)}, bf16[16,672,128]{2,1,0:T(8,128)(2,1)}) fusion(bf16[16,224,128]{2,1,0:T(8,128)(2,1)S(1)} %copy-done.11, bf16[16,448,128]{2,1,0:T(8,128)(2,1)} %bitcast.184, bf16[16,672,128]{2,1,0:T(8,128)(2,1)} %all-to-all-done.5, f32[16,224,128]{2,1,0:T(8,128)} %reshape.137, ...), kind=kLoop, calls=%fused_computation.36 | loop fusion | flops 46792704 | bytes 24772608 | tf_op jit(solution)/shard_map/convert_element_type | solution.py:31
  436.6 37.9 %all_to_all.40 = bf16[16,672,128]{2,1,0:T(8,128)(2,1)S(1)} all-to-all(bf16[16,672,128]{2,1,0:T(8,128)(2,1)S(1)} %get-tuple-element.23), channel_id=1, replica_groups=mesh['expert'=16,'tensor'=8] {'expert'}, dimensions={0} | all-to-all | bytes 5505024 | tf_op jit(solution)/shard_map/all_to_all | solution.py:108
  476.3 5.3 %all-to-all-start.7 = ((bf16[16,672,128]{2,1,0:T(8,128)(2,1)}), bf16[16,672,128]{2,1,0:T(8,128)(2,1)}, u32[]{:S(2)}, u32[]{:S(2)}) async-start(bf16[16,672,128]{2,1,0:T(8,128)(2,1)} %broadcast_select_fusion.1), calls=%async_computation.7 | async-start | bytes 5505024 | tf_op jit(solution)/shard_map/all_to_all | solution.py:108
  481.6 3.0 slice.132
  490.0 1.9 broadcast_in_dim_reshape.27
  491.9 1.9 broadcast_in_dim_reshape.29
  493.9 2.9 broadcast_in_dim_reshape.31
  496.7 18.9 %all-to-all-done.7 = bf16[16,672,128]{2,1,0:T(8,128)(2,1)} async-done(((bf16[16,672,128]{2,1,0:T(8,128)(2,1)}), bf16[16,672,128]{2,1,0:T(8,128)(2,1)}, u32[]{:S(2)}, u32[]{:S(2)}) %all-to-all-start.7) | async-done | bytes 2752544 | tf_op jit(solution)/shard_map/all_to_all | solution.py:108
  516.9 1.9 broadcast_in_dim_reshape.33
  518.8 2.9 slice.138
  (96 shorter events, 29.7 us)
Async XLA Ops:
  0.6 47.3 %copy-start = (bf16[256,3584]{1,0:T(8,128)(2,1)S(1)}, bf16[256,3584]{1,0:T(8,128)(2,1)}, u32[]{:S(2)}) copy-start(bf16[256,3584]{1,0:T(8,128)(2,1)} %param.15) | copy-start | bytes 5505028
  3.1 3.6 copy-start.7
  3.1 10.7 %copy-start.20 = (s32[256,4]{0,1:T(4,128)S(1)}, s32[256,4]{0,1:T(4,128)}, u32[]{:S(2)}) copy-start(s32[256,4]{0,1:T(4,128)} %param.12) | copy-start | bytes 12292
  3.1 11.0 %copy-start.22 = (s32[2]{0:T(128)S(1)}, s32[2]{0:T(128)}, u32[]{:S(2)}) copy-start(s32[2]{0:T(128)} %param.16) | copy-start | bytes 28
  6.7 20.2 %copy-start.21 = (f32[256,4]{0,1:T(4,128)S(1)}, f32[256,4]{0,1:T(4,128)}, u32[]{:S(2)}) copy-start(f32[256,4]{0,1:T(4,128)} %param.13) | copy-start | bytes 12292
  6.7 41.1 %all-to-all-start = ((bf16[16,672,128]{2,1,0:T(8,128)(2,1)}), bf16[16,672,128]{2,1,0:T(8,128)(2,1)}, u32[]{:S(2)}, u32[]{:S(2)}) async-start(bf16[16,672,128]{2,1,0:T(8,128)(2,1)} %pad_maximum_fusion.3), calls=%async_computation | async-start | bytes 5505024 | tf_op jit(solution)/shard_map/all_to_all | solution.py:108
  26.9 8.4 %copy-start.23 = (s32[16]{0:T(128)S(1)}, s32[16]{0:T(128)}, u32[]{:S(2)}) copy-start(s32[16]{0:T(128)} %param.17) | copy-start | bytes 196
  77.6 45.3 %all-to-all-start.2 = ((bf16[16,672,128]{2,1,0:T(8,128)(2,1)}), bf16[16,672,128]{2,1,0:T(8,128)(2,1)}, u32[]{:S(2)}, u32[]{:S(2)}) async-start(bf16[16,672,128]{2,1,0:T(8,128)(2,1)} %broadcast_select_fusion.2), calls=%async_computation.2 | async-start | bytes 5505024 | tf_op jit(solution)/shard_map/all_to_all | solution.py:108
  122.9 108.7 %all-to-all-start.1 = ((bf16[16,2,40,3584]{3,2,1,0:T(8,128)(2,1)}), bf16[16,2,40,3584]{3,2,1,0:T(8,128)(2,1)}, u32[]{:S(2)}, u32[]{:S(2)}) async-start(bf16[16,2,40,3584]{3,2,1,0:T(8,128)(2,1)} %pad_maximum_fusion), calls=%async_computation.1 | async-start | bytes 18350080 | tf_op jit(solution)/shard_map/all_to_all | solution.py:108
  231.5 108.7 %all-to-all-start.3 = ((bf16[16,2,40,3584]{3,2,1,0:T(8,128)(2,1)}), bf16[16,2,40,3584]{3,2,1,0:T(8,128)(2,1)}, u32[]{:S(2)}, u32[]{:S(2)}) async-start(bf16[16,2,40,3584]{3,2,1,0:T(8,128)(2,1)} %pad_maximum_fusion.1), calls=%async_computation.3 | async-start | bytes 18350080 | tf_op jit(solution)/shard_map/all_to_all | solution.py:108
  246.5 2.1 copy-start.4
  246.5 2.1 copy-start.15
  247.9 2.1 copy-start.16
  250.0 5.8 %copy-start.17 = (f32[2,640,128]{2,1,0:T(8,128)S(1)}, f32[2,640,128]{2,1,0:T(8,128)}, u32[]{:S(2)}) copy-start(f32[2,640,128]{2,1,0:T(8,128)} %copy-done.16) | copy-start | bytes 1966084
  261.2 84.2 %copy-start.12 = (bf16[1,128,3584]{2,1,0:T(8,128)(2,1)S(1)}, bf16[1,128,3584]{2,1,0:T(8,128)(2,1)}, u32[]{:S(2)}) copy-start(bf16[1,128,3584]{2,1,0:T(8,128)(2,1)} %param.21) | copy-start | bytes 2752516
  264.1 83.4 %copy-start.13 = (bf16[1,128,3584]{2,1,0:T(8,128)(2,1)S(1)}, bf16[1,128,3584]{2,1,0:T(8,128)(2,1)}, u32[]{:S(2)}) copy-start(bf16[1,128,3584]{2,1,0:T(8,128)(2,1)} %param.23) | copy-start | bytes 2752516
  340.2 39.3 %all-to-all-start.4 = ((bf16[16,672,128]{2,1,0:T(8,128)(2,1)}), bf16[16,672,128]{2,1,0:T(8,128)(2,1)}, u32[]{:S(2)}, u32[]{:S(2)}) async-start(bf16[16,672,128]{2,1,0:T(8,128)(2,1)} %pad_maximum_fusion.5), calls=%async_computation.4 | async-start | bytes 5505024 | tf_op jit(solution)/shard_map/all_to_all | solution.py:108
  384.9 39.6 %all-to-all-start.5 = ((bf16[16,672,128]{2,1,0:T(8,128)(2,1)}), bf16[16,672,128]{2,1,0:T(8,128)(2,1)}, u32[]{:S(2)}, u32[]{:S(2)}) async-start(bf16[16,672,128]{2,1,0:T(8,128)(2,1)} %select_convert_fusion), calls=%async_computation.5 | async-start | bytes 5505024 | tf_op jit(solution)/shard_map/all_to_all | solution.py:108
  390.3 4.4 copy-start.9
  394.7 2.1 copy-start.3
  394.7 2.1 copy-start.14
  396.1 2.0 copy-start.18
  401.6 5.2 %copy-start.19 = (f32[2,640,128]{2,1,0:T(8,128)S(1)}, f32[2,640,128]{2,1,0:T(8,128)}, u32[]{:S(2)}) copy-start(f32[2,640,128]{2,1,0:T(8,128)} %copy-done.18) | copy-start | bytes 1966084
  406.9 17.6 %copy-start.8 = (bf16[16,224,128]{2,1,0:T(8,128)(2,1)S(1)}, bf16[16,224,128]{2,1,0:T(8,128)(2,1)}, u32[]{:S(2)}) copy-start(bf16[16,224,128]{2,1,0:T(8,128)(2,1)} %copy-done.7) | copy-start | bytes 2752516
  406.9 17.6 %copy-start.10 = (bf16[16,224,128]{2,1,0:T(8,128)(2,1)S(1)}, bf16[16,224,128]{2,1,0:T(8,128)(2,1)}, u32[]{:S(2)}) copy-start(bf16[16,224,128]{2,1,0:T(8,128)(2,1)} %reshape_squeeze.33) | copy-start | bytes 2752516
  406.9 17.6 %copy-start.11 = (bf16[16,224,128]{2,1,0:T(8,128)(2,1)S(1)}, bf16[16,224,128]{2,1,0:T(8,128)(2,1)}, u32[]{:S(2)}) copy-start(bf16[16,224,128]{2,1,0:T(8,128)(2,1)} %reshape_squeeze.39) | copy-start | bytes 2752516
  435.0 1.6 copy-start.2
  476.3 39.3 %all-to-all-start.7 = ((bf16[16,672,128]{2,1,0:T(8,128)(2,1)}), bf16[16,672,128]{2,1,0:T(8,128)(2,1)}, u32[]{:S(2)}, u32[]{:S(2)}) async-start(bf16[16,672,128]{2,1,0:T(8,128)(2,1)} %broadcast_select_fusion.1), calls=%async_computation.7 | async-start | bytes 5505024 | tf_op jit(solution)/shard_map/all_to_all | solution.py:108
  481.6 4.4 copy-start.6
  484.7 2.9 copy-start.5
  491.9 29.8 %copy-start.1 = (bf16[256,3584]{1,0:T(8,128)(2,1)S(1)}, bf16[256,3584]{1,0:T(8,128)(2,1)}, u32[]{:S(2)}) copy-start(bf16[256,3584]{1,0:T(8,128)(2,1)} %param.15) | copy-start | bytes 5505028
where the time goes:
time: 531 us; the launch traced here: 522 us
  waiting for transfers between devices  240 us (45%)
  local copies, waits for them, and re-layouts  105 us (20%)
  other arithmetic  74.9 us (14%)
  starting transfers between devices  40 us (8%)
  blocking collectives  37.9 us (7%)
  matrix products  19.7 us (4%)
  between operations  5.51 us (1%)
    all_to_all x7, waiting for transfers between devices, exchange(): return lax.all_to_all(block, 'expert', 0, 0, tiled=True)  240 us
    all_to_all x7, starting transfers between devices, exchange(): return lax.all_to_all(block, 'expert', 0, 0, tiled=True)  40 us
    all_to_all x1, blocking collectives, exchange(): return lax.all_to_all(block, 'expert', 0, 0, tiled=True)  37.9 us
    gather x1, local copies, waits for them, and re-layouts, gather_rows(): tokens[token_index]  18.8 us
    another operation x2, other arithmetic, rows_of(): jnp.stack([built_token[:, add_which], built_cotan[:, add_which]], axis=1)  16.2 us
    slice x1, local copies, waits for them, and re-layouts, rows_of(): built_token[:, add_which]  13.2 us
  transfers between devices with their start and end apart: 7, of which 6 were waited for; matrix products, arithmetic and copies ran while one was open for 26% of the time, Pallas kernels for 0%

commit v1 on v0

--- a/solution.py
+++ b/solution.py
@@ -53,11 +53,20 @@
     return source // top_count, present, weight
 
 
-def gather_rows(token_index, present, weight, tokens, cotangent, slot_count, row_count):
-    rows_token = jnp.where(present[:, None], tokens[token_index], jnp.zeros((), tokens.dtype))
-    rows_cotan = (weight[:, None] * cotangent[token_index].astype(jnp.float32)).astype(jnp.bfloat16)
-    row_shape = (slot_count // 2, 2, row_count, tokens.shape[1])
-    return (rows_token.reshape(row_shape), rows_cotan.reshape(row_shape))
+def gather_rows(row_index, row_scale, tokens, cotangent):
+    source = jnp.concatenate([tokens, cotangent], axis=0)
+    picked = source[row_index].astype(jnp.float32)
+    return (row_scale[..., None] * picked).astype(jnp.bfloat16)
+
+
+def order_rows(token_index, present, weight, expert_count, token_count, capacity):
+    def by_kind(values):
+        return jnp.swapaxes(values.reshape(expert_count, 2, capacity), 0, 1)
+
+    lead = by_kind(token_index)
+    row_index = jnp.stack([lead, lead + token_count], axis=2)
+    row_scale = jnp.stack([by_kind(present.astype(jnp.float32)), by_kind(weight)], axis=2)
+    return row_index, row_scale
 
 
 def slot_terms(rows_token, rows_cotan, weight_in, weight_down, scale_in, scale_down):
@@ -154,20 +163,20 @@
     token_index, present, row_weight = route_rows(
         slot_choices, mix_weights, 2 * expert_count, capacity, capacity
     )
-    first_arrived, token_index, present, row_weight = lax.optimization_barrier(
-        (first_arrived, token_index, present, row_weight)
+    row_index, row_scale = order_rows(
+        token_index, present, row_weight, expert_count, tokens.shape[0], capacity
+    )
+    first_arrived, row_index, row_scale = lax.optimization_barrier(
+        (first_arrived, row_index, row_scale)
     )
     held_in, held_down = unpack(
         spread_chosen(first_arrived, hot_experts, replica_of), width, inner
     )
     weight_sets = ((own_in, own_down), (held_in, held_down))
-    built_token, built_cotan = gather_rows(
-        token_index, present, row_weight, tokens, cotangent, 2 * expert_count, capacity
-    )
+    built_rows = gather_rows(row_index, row_scale, tokens, cotangent)
 
     def rows_of(add_which):
-        outgoing = jnp.stack([built_token[:, add_which], built_cotan[:, add_which]], axis=1)
-        return exchange(outgoing)
+        return exchange(built_rows[add_which])
 
     def terms_of(arrived_rows, add_which):
         return slot_terms(

time: 531 us -> 511 us (0.962)
  blocking collectives: 37.9 us -> 146 us
  waiting for transfers between devices: 240 us -> 144 us
  other arithmetic: 74.9 us -> 53 us
  starting transfers between devices: 40 us -> 32.5 us
    all_to_all x1 -> x2, blocking collectives: 37.9 us -> 146 us  [exchange(): return lax.all_to_all(block, 'expert', 0, 0, tiled=True)]
    all_to_all x7 -> x6, waiting for transfers between devices: 240 us -> 144 us  [exchange(): return lax.all_to_all(block, 'expert', 0, 0, tiled=True)]
    another operation x5 -> x7, other arithmetic: 25.3 us -> 9.23 us  [the longest x2 16.2 us: rows_of(): jnp.stack([built_token[:, add_which], built_cotan[:, add_which]], axis=1)]
    slice x3 -> x2, local copies, waits for them, and re-layouts: 13.4 us -> 0.22 us  [the longest x1 13.2 us: rows_of(): built_token[:, add_which]]
    gather x2 -> x1, local copies, waits for them, and re-layouts: 26.7 us -> 34.9 us  [gather_rows(): picked = source[row_index].astype(jnp.float32)]
    select_n x3 -> x1, other arithmetic: 7.94 us -> 0.02 us  [gather_rows(): picked = source[row_index].astype(jnp.float32)]
    all_to_all x7 -> x6, starting transfers between devices: 40 us -> 32.5 us  [exchange(): return lax.all_to_all(block, 'expert', 0, 0, tiled=True)]
    squeeze x0 -> x1, local copies, waits for them, and re-layouts: none -> 6.66 us  [rows_of(): return exchange(built_rows[add_which])]
  transfers between devices with their start and end apart: 7 -> 6, of which waited for: 6 -> 5; matrix products, arithmetic and copies ran while one was open for 26% -> 27% of each run, Pallas kernels for 0% -> 0%
where the time goes in v1:
time: 511 us; the launch traced here: 502 us
  blocking collectives  146 us (29%)
  waiting for transfers between devices  144 us (28%)
  local copies, waits for them, and re-layouts  102 us (20%)
  other arithmetic  53 us (10%)
  starting transfers between devices  32.5 us (6%)
  matrix products  18 us (4%)
  between operations  5.53 us (1%)
    all_to_all x2, blocking collectives, exchange(): return lax.all_to_all(block, 'expert', 0, 0, tiled=True)  146 us
    all_to_all x6, waiting for transfers between devices, exchange(): return lax.all_to_all(block, 'expert', 0, 0, tiled=True)  144 us
    gather x1, local copies, waits for them, and re-layouts, gather_rows(): picked = source[row_index].astype(jnp.float32)  34.9 us
    all_to_all x6, starting transfers between devices, exchange(): return lax.all_to_all(block, 'expert', 0, 0, tiled=True)  32.5 us
    convert_element_type x1, other arithmetic, adam_step(): second_new.astype(jnp.bfloat16)  11 us
  transfers between devices with their start and end apart: 6, of which 5 were waited for; matrix products, arithmetic and copies ran while one was open for 27% of the time, Pallas kernels for 0%

profile of v1, /device:TPU:1, one launch (start us, length us, event | category | flops | bytes accessed | tf_op | source)
XLA Modules:
  0.0 502.3 jit_solution(9337995797138051519)
XLA Ops:
  0.6 2.3 reshape_squeeze.31
  3.0 3.6 pad_maximum_fusion.2
  6.5 7.0 %all-to-all-start = ((bf16[16,672,128]{2,1,0:T(8,128)(2,1)}), bf16[16,672,128]{2,1,0:T(8,128)(2,1)}, u32[]{:S(2)}, u32[]{:S(2)}) async-start(bf16[16,672,128]{2,1,0:T(8,128)(2,1)} %pad_maximum_fusion.2), calls=%async_computation | async-start | bytes 5505024 | tf_op jit(solution)/shard_map/all_to_all | solution.py:117
  17.2 9.0 %reduce-window.6 = s32[32,8,128]{2,1,0:T(8,128)S(1)} reduce-window(s32[32,8,128]{2,1,0:T(8,128)S(1)} %fusion.58, s32[]{:T(128)} %constant.22.clone.1), window={size=1x1x128 pad=0_0x0_0x127_0}, to_apply=%region_1.2 | reduce-window | flops 4161536 | bytes 262148 | tf_op jit(solution)/shard_map/reduce-window
  28.9 5.0 gather_fusion
  36.9 3.6 pad_maximum_fusion.1
  40.5 7.2 %all-to-all-done = bf16[16,672,128]{2,1,0:T(8,128)(2,1)} async-done(((bf16[16,672,128]{2,1,0:T(8,128)(2,1)}), bf16[16,672,128]{2,1,0:T(8,128)(2,1)}, u32[]{:S(2)}, u32[]{:S(2)}) %all-to-all-start) | async-done | bytes 2752544 | tf_op jit(solution)/shard_map/all_to_all | solution.py:117
  48.9 1.8 broadcast_select_fusion.1
  50.7 4.5 all-to-all-start.2
  55.2 34.9 %gather_fusion.1 = bf16[2560,3584]{1,0:T(8,128)(2,1)} fusion(bf16[512,3584]{1,0:T(8,128)(2,1)} %pad_maximum_fusion.1, s32[3072]{0:T(1024)S(1)} %pad_clamp_fusion), kind=kCustom, calls=%fused_computation.1 | custom fusion | bytes 36710400 | tf_op jit(solution)/shard_map/gather | solution.py:58
  90.1 10.1 %fusion = bf16[2,16,2,40,3584]{4,3,2,1,0:T(8,128)(2,1)S(1)} fusion(bf16[2,16,2,40,3584]{4,3,2,1,0:T(8,128)(2,1)} %bitcast.182, f32[2,16,2,40]{3,2,1,0:T(2,128)S(1)} %copy.70), kind=kLoop, calls=%fused_computation.3 | loop fusion | flops 27525120 | bytes 36710400 | tf_op jit(solution)/shard_map/convert_element_type | solution.py:59
  100.3 6.7 %slice_bitcast_fusion = (bf16[16,2,40,3584]{3,2,1,0:T(8,128)(2,1)}, bf16[16,2,40,3584]{3,2,1,0:T(8,128)(2,1)}) fusion(bf16[2,16,2,40,3584]{4,3,2,1,0:T(8,128)(2,1)S(1)} %fusion), kind=kLoop, calls=%fused_computation.4 | loop fusion | bytes 36700160 | tf_op jit(solution)/shard_map/squeeze | solution.py:179
  107.0 108.6 %all_to_all.40 = bf16[16,2,40,3584]{3,2,1,0:T(8,128)(2,1)} all-to-all(bf16[16,2,40,3584]{3,2,1,0:T(8,128)(2,1)} %get-tuple-element.23), channel_id=1, replica_groups=mesh['expert'=16,'tensor'=8] {'expert'}, dimensions={0} | all-to-all | bytes 18350080 | tf_op jit(solution)/shard_map/all_to_all | solution.py:117
  215.5 5.8 %all-to-all-start.3 = ((bf16[16,2,40,3584]{3,2,1,0:T(8,128)(2,1)}), bf16[16,2,40,3584]{3,2,1,0:T(8,128)(2,1)}, u32[]{:S(2)}, u32[]{:S(2)}) async-start(bf16[16,2,40,3584]{3,2,1,0:T(8,128)(2,1)} %get-tuple-element.22), calls=%async_computation.3 | async-start | bytes 18350080 | tf_op jit(solution)/shard_map/all_to_all | solution.py:117
  222.3 2.9 reshape.126
  225.2 4.4 fusion.66
  231.7 1.5 copy-done.3
  235.4 4.2 fusion.53
  239.6 1.6 fusion.10
  241.3 2.3 copy.75
  243.5 3.2 pad_maximum_fusion.4
  246.7 77.4 %all-to-all-done.3 = bf16[16,2,40,3584]{3,2,1,0:T(8,128)(2,1)} async-done(((bf16[16,2,40,3584]{3,2,1,0:T(8,128)(2,1)}), bf16[16,2,40,3584]{3,2,1,0:T(8,128)(2,1)}, u32[]{:S(2)}, u32[]{:S(2)}) %all-to-all-start.3) | async-done | bytes 9175072 | tf_op jit(solution)/shard_map/all_to_all | solution.py:117
  324.1 4.5 all-to-all-start.4
  328.6 3.0 reshape_squeeze.39
  331.6 3.0 reshape_squeeze.33
  336.6 26.1 %all-to-all-done.4 = bf16[16,672,128]{2,1,0:T(8,128)(2,1)S(1)} async-done(((bf16[16,672,128]{2,1,0:T(8,128)(2,1)}), bf16[16,672,128]{2,1,0:T(8,128)(2,1)S(1)}, u32[]{:S(2)}, u32[]{:S(2)}) %all-to-all-start.4) | async-done | bytes 2752544 | tf_op jit(solution)/shard_map/all_to_all | solution.py:117
  363.9 2.4 select_convert_fusion
  366.3 5.5 %all-to-all-start.5 = ((bf16[16,672,128]{2,1,0:T(8,128)(2,1)}), bf16[16,672,128]{2,1,0:T(8,128)(2,1)}, u32[]{:S(2)}, u32[]{:S(2)}) async-start(bf16[16,672,128]{2,1,0:T(8,128)(2,1)} %select_convert_fusion), calls=%async_computation.5 | async-start | bytes 5505024 | tf_op jit(solution)/shard_map/all_to_all | solution.py:117
  371.8 4.4 fusion.65
  378.3 1.5 copy-done.2
  380.9 1.3 reshape.131
  382.2 4.2 fusion.54
  386.4 3.5 fusion.7
  389.9 5.1 %copy.77 = f32[2,3584,128]{2,1,0:T(8,128)} copy(f32[2,3584,128]{1,2,0:T(8,128)} %fusion.7) | data formatting | bytes 7340032 | tf_op jit(solution)/shard_map/mul | solution.py:201
  395.0 10.8 %all-to-all-done.5 = bf16[16,672,128]{2,1,0:T(8,128)(2,1)} async-done(((bf16[16,672,128]{2,1,0:T(8,128)(2,1)}), bf16[16,672,128]{2,1,0:T(8,128)(2,1)}, u32[]{:S(2)}, u32[]{:S(2)}) %all-to-all-start.5) | async-done | bytes 2752544 | tf_op jit(solution)/shard_map/all_to_all | solution.py:117
  405.8 11.0 %fusion.14 = (bf16[16,672,128]{2,1,0:T(8,128)(2,1)}, bf16[16,672,128]{2,1,0:T(8,128)(2,1)S(1)}, bf16[16,672,128]{2,1,0:T(8,128)(2,1)}) fusion(bf16[16,224,128]{2,1,0:T(8,128)(2,1)} %reshape_squeeze.39, bf16[16,448,128]{2,1,0:T(8,128)(2,1)} %bitcast.204, bf16[16,672,128]{2,1,0:T(8,128)(2,1)} %all-to-all-done.5, f32[16,224,128]{2,1,0:T(8,128)} %reshape.131, ...), kind=kLoop, calls=%fused_computation.35 | loop fusion | flops 46792704 | bytes 24772608 | tf_op jit(solution)/shard_map/convert_element_type | solution.py:31
  416.7 37.9 %all_to_all.41 = bf16[16,672,128]{2,1,0:T(8,128)(2,1)S(1)} all-to-all(bf16[16,672,128]{2,1,0:T(8,128)(2,1)S(1)} %get-tuple-element.25), channel_id=1, replica_groups=mesh['expert'=16,'tensor'=8] {'expert'}, dimensions={0} | all-to-all | bytes 5505024 | tf_op jit(solution)/shard_map/all_to_all | solution.py:117
  454.7 1.8 broadcast_select_fusion
  456.5 5.3 %all-to-all-start.7 = ((bf16[16,672,128]{2,1,0:T(8,128)(2,1)}), bf16[16,672,128]{2,1,0:T(8,128)(2,1)}, u32[]{:S(2)}, u32[]{:S(2)}) async-start(bf16[16,672,128]{2,1,0:T(8,128)(2,1)} %broadcast_select_fusion), calls=%async_computation.7 | async-start | bytes 5505024 | tf_op jit(solution)/shard_map/all_to_all | solution.py:117
  461.8 1.4 slice.120
  464.2 1.4 slice.122
  465.7 1.4 slice.124
  467.2 1.9 broadcast_in_dim_reshape.27
  469.1 1.9 broadcast_in_dim_reshape.29
  471.1 1.9 broadcast_in_dim_reshape.31
  473.0 22.7 %all-to-all-done.7 = bf16[16,672,128]{2,1,0:T(8,128)(2,1)} async-done(((bf16[16,672,128]{2,1,0:T(8,128)(2,1)}), bf16[16,672,128]{2,1,0:T(8,128)(2,1)}, u32[]{:S(2)}, u32[]{:S(2)}) %all-to-all-start.7) | async-done | bytes 2752544 | tf_op jit(solution)/shard_map/all_to_all | solution.py:117
  497.0 1.9 broadcast_in_dim_reshape.33
  499.0 2.9 slice.126
  (96 shorter events, 20.4 us)
Async XLA Ops:
  2.9 3.6 copy-start.7
  2.9 10.7 %copy-start.13 = (s32[256,4]{0,1:T(4,128)S(1)}, s32[256,4]{0,1:T(4,128)}, u32[]{:S(2)}) copy-start(s32[256,4]{0,1:T(4,128)} %param.12) | copy-start | bytes 12292
  2.9 11.0 %copy-start.15 = (s32[2]{0:T(128)S(1)}, s32[2]{0:T(128)}, u32[]{:S(2)}) copy-start(s32[2]{0:T(128)} %param.16) | copy-start | bytes 28
  6.5 21.3 %copy-start.14 = (f32[256,4]{0,1:T(4,128)S(1)}, f32[256,4]{0,1:T(4,128)}, u32[]{:S(2)}) copy-start(f32[256,4]{0,1:T(4,128)} %param.13) | copy-start | bytes 12292
  6.5 41.1 %all-to-all-start = ((bf16[16,672,128]{2,1,0:T(8,128)(2,1)}), bf16[16,672,128]{2,1,0:T(8,128)(2,1)}, u32[]{:S(2)}, u32[]{:S(2)}) async-start(bf16[16,672,128]{2,1,0:T(8,128)(2,1)} %pad_maximum_fusion.2), calls=%async_computation | async-start | bytes 5505024 | tf_op jit(solution)/shard_map/all_to_all | solution.py:117
  26.8 8.7 %copy-start.16 = (s32[16]{0:T(128)S(1)}, s32[16]{0:T(128)}, u32[]{:S(2)}) copy-start(s32[16]{0:T(128)} %param.17) | copy-start | bytes 196
  26.8 10.0 %copy-start.10 = (bf16[256,3584]{1,0:T(8,128)(2,1)S(1)}, bf16[256,3584]{1,0:T(8,128)(2,1)}, u32[]{:S(2)}) copy-start(bf16[256,3584]{1,0:T(8,128)(2,1)} %param.15) | copy-start | bytes 5505028
  50.7 56.2 %all-to-all-start.2 = ((bf16[16,672,128]{2,1,0:T(8,128)(2,1)}), bf16[16,672,128]{2,1,0:T(8,128)(2,1)S(1)}, u32[]{:S(2)}, u32[]{:S(2)}) async-start(bf16[16,672,128]{2,1,0:T(8,128)(2,1)} %broadcast_select_fusion.1), calls=%async_computation.2 | async-start | bytes 5505024 | tf_op jit(solution)/shard_map/all_to_all | solution.py:117
  107.0 118.2 %copy-start.4 = (bf16[16,672,128]{2,1,0:T(8,128)(2,1)}, bf16[16,672,128]{2,1,0:T(8,128)(2,1)S(1)}, u32[]{:S(2)}) copy-start(bf16[16,672,128]{2,1,0:T(8,128)(2,1)S(1)} %all-to-all-done.2) | copy-start | bytes 8257540
  215.5 108.6 %all-to-all-start.3 = ((bf16[16,2,40,3584]{3,2,1,0:T(8,128)(2,1)}), bf16[16,2,40,3584]{3,2,1,0:T(8,128)(2,1)}, u32[]{:S(2)}, u32[]{:S(2)}) async-start(bf16[16,2,40,3584]{3,2,1,0:T(8,128)(2,1)} %get-tuple-element.22), calls=%async_computation.3 | async-start | bytes 18350080 | tf_op jit(solution)/shard_map/all_to_all | solution.py:117
  225.2 4.4 slice-start.4
  229.6 2.2 copy-start.1
  229.6 3.6 copy-start.3
  231.7 1.6 copy-start.11
  234.2 5.4 %slice-start.2 = ((s8[4587520]{0:T(1024)(128)(4,1)}), s8[393216]{0:T(1024)(128)(4,1)S(1)}, s32[]{:S(2)}) async-start(s8[4587520]{0:T(1024)(128)(4,1)} %bitcast.188), calls=%async_computation.10 | async-start | bytes 786432
  235.4 4.2 slice-start.3
  324.1 38.6 %all-to-all-start.4 = ((bf16[16,672,128]{2,1,0:T(8,128)(2,1)}), bf16[16,672,128]{2,1,0:T(8,128)(2,1)S(1)}, u32[]{:S(2)}, u32[]{:S(2)}) async-start(bf16[16,672,128]{2,1,0:T(8,128)(2,1)} %pad_maximum_fusion.4), calls=%async_computation.4 | async-start | bytes 5505024 | tf_op jit(solution)/shard_map/all_to_all | solution.py:117
  366.3 39.5 %all-to-all-start.5 = ((bf16[16,672,128]{2,1,0:T(8,128)(2,1)}), bf16[16,672,128]{2,1,0:T(8,128)(2,1)}, u32[]{:S(2)}, u32[]{:S(2)}) async-start(bf16[16,672,128]{2,1,0:T(8,128)(2,1)} %select_convert_fusion), calls=%async_computation.5 | async-start | bytes 5505024 | tf_op jit(solution)/shard_map/all_to_all | solution.py:117
  371.8 4.4 copy-start.8
  376.2 2.1 copy-start
  376.2 3.5 copy-start.2
  378.3 1.6 copy-start.12
  380.9 5.6 %slice-start = ((s8[4587520]{0:T(1024)(128)(4,1)}), s8[393216]{0:T(1024)(128)(4,1)S(1)}, s32[]{:S(2)}) async-start(s8[4587520]{0:T(1024)(128)(4,1)} %bitcast.184), calls=%async_computation.8 | async-start | bytes 786432
  382.2 4.2 slice-start.1
  456.5 39.3 %all-to-all-start.7 = ((bf16[16,672,128]{2,1,0:T(8,128)(2,1)}), bf16[16,672,128]{2,1,0:T(8,128)(2,1)}, u32[]{:S(2)}, u32[]{:S(2)}) async-start(bf16[16,672,128]{2,1,0:T(8,128)(2,1)} %broadcast_select_fusion), calls=%async_computation.7 | async-start | bytes 5505024 | tf_op jit(solution)/shard_map/all_to_all | solution.py:117
  461.8 2.4 copy-start.6
  463.2 2.5 copy-start.5
  465.6 1.6 copy-start.9

commit v2 on v1

--- a/solution.py
+++ b/solution.py
@@ -55,8 +55,13 @@
 
 def gather_rows(row_index, row_scale, tokens, cotangent):
     source = jnp.concatenate([tokens, cotangent], axis=0)
-    picked = source[row_index].astype(jnp.float32)
-    return (row_scale[..., None] * picked).astype(jnp.bfloat16)
+    flat_index = row_index.reshape(-1)
+    choose = (
+        flat_index[:, None] == jnp.arange(source.shape[0], dtype=jnp.int32)[None, :]
+    ).astype(source.dtype)
+    picked = jnp.dot(choose, source, preferred_element_type=jnp.float32)
+    scaled = row_scale.reshape(-1)[:, None] * picked
+    return scaled.astype(jnp.bfloat16).reshape(row_index.shape + (source.shape[1],))
 
 
 def order_rows(token_index, present, weight, expert_count, token_count, capacity):
@@ -169,14 +174,16 @@
     first_arrived, row_index, row_scale = lax.optimization_barrier(
         (first_arrived, row_index, row_scale)
     )
-    held_in, held_down = unpack(
-        spread_chosen(first_arrived, hot_experts, replica_of), width, inner
-    )
-    weight_sets = ((own_in, own_down), (held_in, held_down))
+    held_packed = spread_chosen(first_arrived, hot_experts, replica_of)
     built_rows = gather_rows(row_index, row_scale, tokens, cotangent)
 
     def rows_of(add_which):
         return exchange(built_rows[add_which])
+
+    copy_rows = rows_of(1)
+    copy_rows, held_packed = lax.optimization_barrier((copy_rows, held_packed))
+    held_in, held_down = unpack(held_packed, width, inner)
+    weight_sets = ((own_in, own_down), (held_in, held_down))
 
     def terms_of(arrived_rows, add_which):
         return slot_terms(
@@ -188,7 +195,6 @@
             scale_down,
         )
 
-    copy_rows = rows_of(1)
     copy_in, copy_down = terms_of(copy_rows, 1)
     own_rows = rows_of(0)
     copy_packed = pack(

time: 511 us -> 485 us (0.949); the launches traced: 502 us -> 484 us
  local copies, waits for them, and re-layouts: 102 us -> 66.8 us
  waiting for transfers between devices: 144 us -> 164 us
  other arithmetic: 53 us -> 38.8 us
  matrix products: 18 us -> 30.5 us
    gather x1 -> x0, local copies, waits for them, and re-layouts: 34.9 us -> none  [gather_rows(): picked = source[row_index].astype(jnp.float32)]
    all_to_all x6, waiting for transfers between devices: 144 us -> 164 us  [exchange(): return lax.all_to_all(block, 'expert', 0, 0, tiled=True)]
    dot_general x0 -> x1, matrix products: none -> 12.3 us  [gather_rows(): picked = jnp.dot(choose, source, preferred_element_type=jnp.float32)]
    convert_element_type x1 -> x0, other arithmetic: 10.1 us -> none  [gather_rows(): return (row_scale[..., None] * picked).astype(jnp.bfloat16)]
    squeeze x1 -> x0, local copies, waits for them, and re-layouts: 6.66 us -> none  [rows_of(): return exchange(built_rows[add_which])]
    slice x2 -> x3, local copies, waits for them, and re-layouts: 0.22 us -> 6.72 us  [the longest x1 6.5 us: rows_of(): return exchange(built_rows[add_which])]
    dot_general x2, matrix products: 8.38 us -> 2.7 us  [slot_terms(): jnp.einsum('rd,fd->rf', rows_cotan, weight_down, preferred_element_type=j...]
  transfers between devices with their start and end apart: 6 -> 6, of which waited for: 5 -> 6; matrix products, arithmetic and copies ran while one was open for 27% -> 21% of each run, Pallas kernels for 0% -> 0%
where the time goes in v2:
time: 485 us; the launch traced here: 484 us
  waiting for transfers between devices  164 us (34%)
  blocking collectives  146 us (30%)
  local copies, waits for them, and re-layouts  66.8 us (14%)
  other arithmetic  38.8 us (8%)
  starting transfers between devices  32.2 us (7%)
  matrix products  30.5 us (6%)
  between operations  5.02 us (1%)
    all_to_all x6, waiting for transfers between devices, exchange(): return lax.all_to_all(block, 'expert', 0, 0, tiled=True)  164 us
    all_to_all x2, blocking collectives, exchange(): return lax.all_to_all(block, 'expert', 0, 0, tiled=True)  146 us
    all_to_all x6, starting transfers between devices, exchange(): return lax.all_to_all(block, 'expert', 0, 0, tiled=True)  32.2 us
    dot_general x1, matrix products, gather_rows(): picked = jnp.dot(choose, source, preferred_element_type=jnp.float32)  12.3 us
    convert_element_type x1, other arithmetic, adam_step(): second_new.astype(jnp.bfloat16)  10.9 us
  transfers between devices with their start and end apart: 6, of which 6 were waited for; matrix products, arithmetic and copies ran while one was open for 21% of the time, Pallas kernels for 0%

profile of v2, /device:TPU:1, one launch (start us, length us, event | category | flops | bytes accessed | tf_op | source)
XLA Modules:
  0.0 483.8 jit_solution(15058825883839063937)
XLA Ops:
  0.6 2.3 reshape_squeeze.31
  3.0 3.6 pad_maximum_fusion.1
  6.6 7.0 %all-to-all-start = ((bf16[16,672,128]{2,1,0:T(8,128)(2,1)}), bf16[16,672,128]{2,1,0:T(8,128)(2,1)}, u32[]{:S(2)}, u32[]{:S(2)}) async-start(bf16[16,672,128]{2,1,0:T(8,128)(2,1)} %pad_maximum_fusion.1), calls=%async_computation | async-start | bytes 5505024 | tf_op jit(solution)/shard_map/all_to_all | solution.py:122
  17.2 9.0 %reduce-window.6 = s32[32,8,128]{2,1,0:T(8,128)S(1)} reduce-window(s32[32,8,128]{2,1,0:T(8,128)S(1)} %fusion.61, s32[]{:T(128)} %constant.29.clone.1), window={size=1x1x128 pad=0_0x0_0x127_0}, to_apply=%region_1.2 | reduce-window | flops 4161536 | bytes 262148 | tf_op jit(solution)/shard_map/reduce-window
  29.0 5.0 %gather_fusion = f32[1280]{0:T(1024)S(1)} fusion(f32[1024]{0:T(1024)S(1)} %reshape.131, s32[2048]{0:T(1024)S(1)} %pad_clamp_fusion), kind=kCustom, calls=%fused_computation | custom fusion | bytes 15360 | tf_op jit(solution)/shard_map/gather | solution.py:52
  36.9 10.8 %all-to-all-done = bf16[16,672,128]{2,1,0:T(8,128)(2,1)} async-done(((bf16[16,672,128]{2,1,0:T(8,128)(2,1)}), bf16[16,672,128]{2,1,0:T(8,128)(2,1)}, u32[]{:S(2)}, u32[]{:S(2)}) %all-to-all-start) | async-done | bytes 2752544 | tf_op jit(solution)/shard_map/all_to_all | solution.py:122
  48.7 1.8 broadcast_select_fusion.1
  50.5 5.2 %all-to-all-start.2 = ((bf16[16,672,128]{2,1,0:T(8,128)(2,1)}), bf16[16,672,128]{2,1,0:T(8,128)(2,1)}, u32[]{:S(2)}, u32[]{:S(2)}) async-start(bf16[16,672,128]{2,1,0:T(8,128)(2,1)} %broadcast_select_fusion.1), calls=%async_computation.2 | async-start | bytes 5505024 | tf_op jit(solution)/shard_map/all_to_all | solution.py:122
  56.0 12.3 %multiply_convert_fusion = bf16[2560,3584]{1,0:T(8,128)(2,1)S(1)} fusion(f32[2560]{0:T(1024)S(1)} %mul.158, bf16[256,3584]{1,0:T(8,128)(2,1)S(1)} %copy-done.17, bf16[256,3584]{1,0:T(8,128)(2,1)} %param.14, s32[2560]{0:T(1024)S(1)} %eq.101), kind=kOutput, calls=%fused_computation.1 | convolution fusion | flops 9422241792 | bytes 22040576 | tf_op jit(solution)/shard_map/dot_general | solution.py:62
  68.3 6.5 %fusion.69 = (bf16[1280,3584]{1,0:T(8,128)(2,1)}, bf16[1280,3584]{1,0:T(8,128)(2,1)}) fusion(bf16[2560,3584]{1,0:T(8,128)(2,1)S(1)} %multiply_convert_fusion), kind=kLoop, calls=%fused_computation.128 | loop fusion | bytes 36700160 | tf_op jit(solution)/shard_map/slice | solution.py:181
  74.8 15.1 %all-to-all-done.2 = bf16[16,672,128]{2,1,0:T(8,128)(2,1)} async-done(((bf16[16,672,128]{2,1,0:T(8,128)(2,1)}), bf16[16,672,128]{2,1,0:T(8,128)(2,1)}, u32[]{:S(2)}, u32[]{:S(2)}) %all-to-all-start.2) | async-done | bytes 2752544 | tf_op jit(solution)/shard_map/all_to_all | solution.py:122
  89.9 108.3 %all_to_all.40 = bf16[16,2,40,3584]{3,2,1,0:T(8,128)(2,1)} all-to-all(bf16[16,2,40,3584]{3,2,1,0:T(8,128)(2,1)} %bitcast.179), channel_id=1, replica_groups=mesh['expert'=16,'tensor'=8] {'expert'}, dimensions={0} | all-to-all | bytes 18350080 | tf_op jit(solution)/shard_map/all_to_all | solution.py:122
  198.1 5.5 %all-to-all-start.3 = ((bf16[16,2,40,3584]{3,2,1,0:T(8,128)(2,1)}), bf16[16,2,40,3584]{3,2,1,0:T(8,128)(2,1)}, u32[]{:S(2)}, u32[]{:S(2)}) async-start(bf16[16,2,40,3584]{3,2,1,0:T(8,128)(2,1)} %bitcast.178), calls=%async_computation.3 | async-start | bytes 18350080 | tf_op jit(solution)/shard_map/all_to_all | solution.py:122
  203.6 1.6 slice.89
  206.5 1.9 reshape.132
  208.4 4.3 fusion.71
  214.9 1.4 fusion.56
  216.2 2.9 fusion.9
  219.1 2.9 copy.58
  222.0 3.2 fusion.10
  225.3 2.1 reshape.135
  227.4 2.9 pad_maximum_fusion.3
  230.2 76.4 %all-to-all-done.3 = bf16[16,2,40,3584]{3,2,1,0:T(8,128)(2,1)} async-done(((bf16[16,2,40,3584]{3,2,1,0:T(8,128)(2,1)}), bf16[16,2,40,3584]{3,2,1,0:T(8,128)(2,1)}, u32[]{:S(2)}, u32[]{:S(2)}) %all-to-all-start.3) | async-done | bytes 9175072 | tf_op jit(solution)/shard_map/all_to_all | solution.py:122
  306.6 4.5 all-to-all-start.4
  311.1 3.0 reshape_squeeze.33
  314.1 3.0 reshape_squeeze.39
  319.0 26.1 %all-to-all-done.4 = bf16[16,672,128]{2,1,0:T(8,128)(2,1)S(1)} async-done(((bf16[16,672,128]{2,1,0:T(8,128)(2,1)}), bf16[16,672,128]{2,1,0:T(8,128)(2,1)S(1)}, u32[]{:S(2)}, u32[]{:S(2)}) %all-to-all-start.4) | async-done | bytes 2752544 | tf_op jit(solution)/shard_map/all_to_all | solution.py:122
  346.3 2.3 select_convert_fusion
  348.6 5.2 %all-to-all-start.5 = ((bf16[16,672,128]{2,1,0:T(8,128)(2,1)}), bf16[16,672,128]{2,1,0:T(8,128)(2,1)}, u32[]{:S(2)}, u32[]{:S(2)}) async-start(bf16[16,672,128]{2,1,0:T(8,128)(2,1)} %select_convert_fusion), calls=%async_computation.5 | async-start | bytes 5505024 | tf_op jit(solution)/shard_map/all_to_all | solution.py:122
  353.8 4.4 fusion.70
  361.7 3.5 fusion.6
  365.2 5.2 %copy.60 = f32[2,3584,128]{2,1,0:T(8,128)} copy(f32[2,3584,128]{1,2,0:T(8,128)} %fusion.6) | data formatting | bytes 7340032 | tf_op jit(solution)/shard_map/mul | solution.py:207
  370.4 3.2 convolution_multiply_fusion.2
  373.6 1.3 reshape.137
  375.0 13.0 %all-to-all-done.5 = bf16[16,672,128]{2,1,0:T(8,128)(2,1)} async-done(((bf16[16,672,128]{2,1,0:T(8,128)(2,1)}), bf16[16,672,128]{2,1,0:T(8,128)(2,1)}, u32[]{:S(2)}, u32[]{:S(2)}) %all-to-all-start.5) | async-done | bytes 2752544 | tf_op jit(solution)/shard_map/all_to_all | solution.py:122
  388.0 10.9 %fusion.16 = (bf16[16,672,128]{2,1,0:T(8,128)(2,1)}, bf16[16,672,128]{2,1,0:T(8,128)(2,1)S(1)}, bf16[16,672,128]{2,1,0:T(8,128)(2,1)}) fusion(bf16[16,224,128]{2,1,0:T(8,128)(2,1)} %reshape_squeeze.39, bf16[16,448,128]{2,1,0:T(8,128)(2,1)} %bitcast.197, bf16[16,672,128]{2,1,0:T(8,128)(2,1)} %all-to-all-done.5, f32[16,224,128]{2,1,0:T(8,128)} %reshape.137, ...), kind=kLoop, calls=%fused_computation.34 | loop fusion | flops 46792704 | bytes 24772608 | tf_op jit(solution)/shard_map/convert_element_type | solution.py:31
  398.9 37.9 %all_to_all.41 = bf16[16,672,128]{2,1,0:T(8,128)(2,1)S(1)} all-to-all(bf16[16,672,128]{2,1,0:T(8,128)(2,1)S(1)} %get-tuple-element.29), channel_id=1, replica_groups=mesh['expert'=16,'tensor'=8] {'expert'}, dimensions={0} | all-to-all | bytes 5505024 | tf_op jit(solution)/shard_map/all_to_all | solution.py:122
  436.8 1.9 broadcast_select_fusion
  438.7 4.9 %all-to-all-start.7 = ((bf16[16,672,128]{2,1,0:T(8,128)(2,1)}), bf16[16,672,128]{2,1,0:T(8,128)(2,1)}, u32[]{:S(2)}, u32[]{:S(2)}) async-start(bf16[16,672,128]{2,1,0:T(8,128)(2,1)} %broadcast_select_fusion), calls=%async_computation.7 | async-start | bytes 5505024 | tf_op jit(solution)/shard_map/all_to_all | solution.py:122
  443.6 1.4 slice.116
  446.0 1.4 slice.118
  447.5 1.4 slice.120
  449.0 1.9 broadcast_in_dim_reshape.29
  450.9 1.9 broadcast_in_dim_reshape.31
  452.9 1.9 broadcast_in_dim_reshape.33
  454.8 22.9 %all-to-all-done.7 = bf16[16,672,128]{2,1,0:T(8,128)(2,1)} async-done(((bf16[16,672,128]{2,1,0:T(8,128)(2,1)}), bf16[16,672,128]{2,1,0:T(8,128)(2,1)}, u32[]{:S(2)}, u32[]{:S(2)}) %all-to-all-start.7) | async-done | bytes 2752544 | tf_op jit(solution)/shard_map/all_to_all | solution.py:122
  479.0 1.9 broadcast_in_dim_reshape.35
  480.9 2.9 slice.122
  (84 shorter events, 18.8 us)
Async XLA Ops:
  2.9 3.6 copy-start.4
  2.9 10.7 %copy-start.15 = (s32[2]{0:T(128)S(1)}, s32[2]{0:T(128)}, u32[]{:S(2)}) copy-start(s32[2]{0:T(128)} %param.16) | copy-start | bytes 28
  2.9 11.2 %copy-start.13 = (s32[256,4]{0,1:T(4,128)S(1)}, s32[256,4]{0,1:T(4,128)}, u32[]{:S(2)}) copy-start(s32[256,4]{0,1:T(4,128)} %param.12) | copy-start | bytes 12292
  6.6 20.2 %copy-start.14 = (f32[256,4]{0,1:T(4,128)S(1)}, f32[256,4]{0,1:T(4,128)}, u32[]{:S(2)}) copy-start(f32[256,4]{0,1:T(4,128)} %param.13) | copy-start | bytes 12292
  6.6 41.1 %all-to-all-start = ((bf16[16,672,128]{2,1,0:T(8,128)(2,1)}), bf16[16,672,128]{2,1,0:T(8,128)(2,1)}, u32[]{:S(2)}, u32[]{:S(2)}) async-start(bf16[16,672,128]{2,1,0:T(8,128)(2,1)} %pad_maximum_fusion.1), calls=%async_computation | async-start | bytes 5505024 | tf_op jit(solution)/shard_map/all_to_all | solution.py:122
  27.0 8.5 %copy-start.16 = (s32[16]{0:T(128)S(1)}, s32[16]{0:T(128)}, u32[]{:S(2)}) copy-start(s32[16]{0:T(128)} %param.17) | copy-start | bytes 196
  36.9 19.1 %copy-start.17 = (bf16[256,3584]{1,0:T(8,128)(2,1)S(1)}, bf16[256,3584]{1,0:T(8,128)(2,1)}, u32[]{:S(2)}) copy-start(bf16[256,3584]{1,0:T(8,128)(2,1)} %param.15) | copy-start | bytes 5505028
  50.5 39.4 %all-to-all-start.2 = ((bf16[16,672,128]{2,1,0:T(8,128)(2,1)}), bf16[16,672,128]{2,1,0:T(8,128)(2,1)}, u32[]{:S(2)}, u32[]{:S(2)}) async-start(bf16[16,672,128]{2,1,0:T(8,128)(2,1)} %broadcast_select_fusion.1), calls=%async_computation.2 | async-start | bytes 5505024 | tf_op jit(solution)/shard_map/all_to_all | solution.py:122
  198.1 108.4 %all-to-all-start.3 = ((bf16[16,2,40,3584]{3,2,1,0:T(8,128)(2,1)}), bf16[16,2,40,3584]{3,2,1,0:T(8,128)(2,1)}, u32[]{:S(2)}, u32[]{:S(2)}) async-start(bf16[16,2,40,3584]{3,2,1,0:T(8,128)(2,1)} %bitcast.178), calls=%async_computation.3 | async-start | bytes 18350080 | tf_op jit(solution)/shard_map/all_to_all | solution.py:122
  212.7 2.2 copy-start.1
  212.7 2.1 copy-start.8
  214.1 2.1 copy-start.9
  216.2 5.8 %copy-start.10 = (f32[2,640,128]{2,1,0:T(8,128)S(1)}, f32[2,640,128]{2,1,0:T(8,128)}, u32[]{:S(2)}) copy-start(f32[2,640,128]{2,1,0:T(8,128)} %copy-done.9) | copy-start | bytes 1966084
  306.6 38.6 %all-to-all-start.4 = ((bf16[16,672,128]{2,1,0:T(8,128)(2,1)}), bf16[16,672,128]{2,1,0:T(8,128)(2,1)S(1)}, u32[]{:S(2)}, u32[]{:S(2)}) async-start(bf16[16,672,128]{2,1,0:T(8,128)(2,1)} %pad_maximum_fusion.3), calls=%async_computation.4 | async-start | bytes 5505024 | tf_op jit(solution)/shard_map/all_to_all | solution.py:122
  348.6 39.3 %all-to-all-start.5 = ((bf16[16,672,128]{2,1,0:T(8,128)(2,1)}), bf16[16,672,128]{2,1,0:T(8,128)(2,1)}, u32[]{:S(2)}, u32[]{:S(2)}) async-start(bf16[16,672,128]{2,1,0:T(8,128)(2,1)} %select_convert_fusion), calls=%async_computation.5 | async-start | bytes 5505024 | tf_op jit(solution)/shard_map/all_to_all | solution.py:122
  353.8 4.4 copy-start.5
  358.2 2.1 copy-start
  358.3 2.1 copy-start.7
  359.6 2.1 copy-start.11
  365.2 5.2 %copy-start.12 = (f32[2,640,128]{2,1,0:T(8,128)S(1)}, f32[2,640,128]{2,1,0:T(8,128)}, u32[]{:S(2)}) copy-start(f32[2,640,128]{2,1,0:T(8,128)} %copy-done.11) | copy-start | bytes 1966084
  438.7 39.0 %all-to-all-start.7 = ((bf16[16,672,128]{2,1,0:T(8,128)(2,1)}), bf16[16,672,128]{2,1,0:T(8,128)(2,1)}, u32[]{:S(2)}, u32[]{:S(2)}) async-start(bf16[16,672,128]{2,1,0:T(8,128)(2,1)} %broadcast_select_fusion), calls=%async_computation.7 | async-start | bytes 5505024 | tf_op jit(solution)/shard_map/all_to_all | solution.py:122
  443.6 2.4 copy-start.3
  445.0 2.5 copy-start.2
  447.4 1.6 copy-start.6

commit v3 on v2

--- a/solution.py
+++ b/solution.py
@@ -174,7 +174,15 @@
     first_arrived, row_index, row_scale = lax.optimization_barrier(
         (first_arrived, row_index, row_scale)
     )
-    held_packed = spread_chosen(first_arrived, hot_experts, replica_of)
+    both_hot = jnp.stack(
+        [
+            lax.dynamic_index_in_dim(first_arrived, hot_experts[which], 0, keepdims=False)
+            for which in range(2)
+        ]
+    )
+    every_chunk = lax.all_gather(both_hot, "expert", axis=0)
+    wanted_hot = (replica_of[own_index] == hot_experts[1]).astype(jnp.int32)
+    held_packed = lax.dynamic_index_in_dim(every_chunk, wanted_hot, 1, keepdims=False)
     built_rows = gather_rows(row_index, row_scale, tokens, cotangent)
 
     def rows_of(add_which):

time: 485 us -> 518 us (1.068)
  waiting for transfers between devices: 164 us -> 290 us
  blocking collectives: 146 us -> 37.9 us
  between operations: 5.02 us -> 19.7 us
    all_to_all x6, waiting for transfers between devices: 164 us -> 290 us  [exchange(): return lax.all_to_all(block, 'expert', 0, 0, tiled=True)]
    all_to_all x2 -> x1, blocking collectives: 146 us -> 37.9 us  [exchange(): return lax.all_to_all(block, 'expert', 0, 0, tiled=True)]
  transfers between devices with their start and end apart: 6 -> 7, of which waited for: 6 -> 6; matrix products, arithmetic and copies ran while one was open for 21% -> 17% of each run, Pallas kernels for 0% -> 0%
where the time goes in v3:
time: 518 us; the launch traced here: 517 us
  waiting for transfers between devices  290 us (56%)
  local copies, waits for them, and re-layouts  68.2 us (13%)
  blocking collectives  37.9 us (7%)
  other arithmetic  37.1 us (7%)
  starting transfers between devices  32.8 us (6%)
  matrix products  30.5 us (6%)
  between operations  19.7 us (4%)
    all_to_all x6, waiting for transfers between devices, exchange(): return lax.all_to_all(block, 'expert', 0, 0, tiled=True)  290 us
    all_to_all x1, blocking collectives, exchange(): return lax.all_to_all(block, 'expert', 0, 0, tiled=True)  37.9 us
    all_to_all x6, starting transfers between devices, exchange(): return lax.all_to_all(block, 'expert', 0, 0, tiled=True)  32.8 us
    dot_general x1, matrix products, gather_rows(): picked = jnp.dot(choose, source, preferred_element_type=jnp.float32)  12.3 us
    convert_element_type x1, other arithmetic, adam_step(): second_new.astype(jnp.bfloat16)  10.9 us
  transfers between devices with their start and end apart: 7, of which 6 were waited for; matrix products, arithmetic and copies ran while one was open for 17% of the time, Pallas kernels for 0%

profile of v3, /device:TPU:1, one launch (start us, length us, event | category | flops | bytes accessed | tf_op | source)
XLA Modules:
  0.0 516.6 jit_solution(12055214370086616073)
XLA Ops:
  7.2 2.3 reshape_squeeze.31
  9.5 3.6 pad_maximum_fusion.1
  13.1 7.0 %all-to-all-start = ((bf16[16,672,128]{2,1,0:T(8,128)(2,1)}), bf16[16,672,128]{2,1,0:T(8,128)(2,1)}, u32[]{:S(2)}, u32[]{:S(2)}) async-start(bf16[16,672,128]{2,1,0:T(8,128)(2,1)} %pad_maximum_fusion.1), calls=%async_computation | async-start | bytes 5505024 | tf_op jit(solution)/shard_map/all_to_all | solution.py:122
  20.5 9.0 %reduce-window.6 = s32[32,8,128]{2,1,0:T(8,128)S(1)} reduce-window(s32[32,8,128]{2,1,0:T(8,128)S(1)} %fusion.61, s32[]{:T(128)} %constant.33.clone.1), window={size=1x1x128 pad=0_0x0_0x127_0}, to_apply=%region_1.2 | reduce-window | flops 4161536 | bytes 262148 | tf_op jit(solution)/shard_map/reduce-window
  32.3 5.0 gather_fusion
  37.6 16.6 %all-to-all-done = bf16[16,672,128]{2,1,0:T(8,128)(2,1)} async-done(((bf16[16,672,128]{2,1,0:T(8,128)(2,1)}), bf16[16,672,128]{2,1,0:T(8,128)(2,1)}, u32[]{:S(2)}, u32[]{:S(2)}) %all-to-all-start) | async-done | bytes 2752544 | tf_op jit(solution)/shard_map/all_to_all | solution.py:122
  54.4 12.3 %multiply_convert_fusion = bf16[2560,3584]{1,0:T(8,128)(2,1)S(1)} fusion(f32[2560]{0:T(1024)S(1)} %mul.158, bf16[256,3584]{1,0:T(8,128)(2,1)S(1)} %copy-done.18, bf16[256,3584]{1,0:T(8,128)(2,1)} %param.14, s32[2560]{0:T(1024)S(1)} %eq.102), kind=kOutput, calls=%fused_computation.1 | convolution fusion | flops 9422241792 | bytes 22040576 | tf_op jit(solution)/shard_map/dot_general | solution.py:62
  66.7 6.5 %fusion.69 = (bf16[1280,3584]{1,0:T(8,128)(2,1)}, bf16[1280,3584]{1,0:T(8,128)(2,1)}) fusion(bf16[2560,3584]{1,0:T(8,128)(2,1)S(1)} %multiply_convert_fusion), kind=kLoop, calls=%fused_computation.129 | loop fusion | bytes 36700160 | tf_op jit(solution)/shard_map/slice | solution.py:189
  73.2 5.6 %all-to-all-start.1 = ((bf16[16,2,40,3584]{3,2,1,0:T(8,128)(2,1)}), bf16[16,2,40,3584]{3,2,1,0:T(8,128)(2,1)}, u32[]{:S(2)}, u32[]{:S(2)}) async-start(bf16[16,2,40,3584]{3,2,1,0:T(8,128)(2,1)} %bitcast.181), calls=%async_computation.1 | async-start | bytes 18350080 | tf_op jit(solution)/shard_map/all_to_all | solution.py:122
  85.2 138.8 %all-to-all-done.1 = bf16[16,2,40,3584]{3,2,1,0:T(8,128)(2,1)} async-done(((bf16[16,2,40,3584]{3,2,1,0:T(8,128)(2,1)}), bf16[16,2,40,3584]{3,2,1,0:T(8,128)(2,1)}, u32[]{:S(2)}, u32[]{:S(2)}) %all-to-all-start.1) | async-done | bytes 9175072 | tf_op jit(solution)/shard_map/all_to_all | solution.py:122
  224.0 5.6 %all-to-all-start.2 = ((bf16[16,2,40,3584]{3,2,1,0:T(8,128)(2,1)}), bf16[16,2,40,3584]{3,2,1,0:T(8,128)(2,1)}, u32[]{:S(2)}, u32[]{:S(2)}) async-start(bf16[16,2,40,3584]{3,2,1,0:T(8,128)(2,1)} %bitcast.180), calls=%async_computation.2 | async-start | bytes 18350080 | tf_op jit(solution)/shard_map/all_to_all | solution.py:122
  231.5 2.0 dynamic-slice_bitcast_fusion
  233.5 1.6 copy-done.2
  235.2 1.9 reshape.132
  237.1 4.4 fusion.71
  243.7 1.4 fusion.56
  245.1 2.9 fusion.9
  247.9 2.9 copy.75
  250.8 3.2 fusion.10
  254.1 2.1 reshape.135
  256.2 2.9 pad_maximum_fusion.3
  259.0 73.5 %all-to-all-done.2 = bf16[16,2,40,3584]{3,2,1,0:T(8,128)(2,1)} async-done(((bf16[16,2,40,3584]{3,2,1,0:T(8,128)(2,1)}), bf16[16,2,40,3584]{3,2,1,0:T(8,128)(2,1)}, u32[]{:S(2)}, u32[]{:S(2)}) %all-to-all-start.2) | async-done | bytes 9175072 | tf_op jit(solution)/shard_map/all_to_all | solution.py:122
  332.6 4.5 all-to-all-start.3
  337.0 3.0 reshape_squeeze.33
  340.0 3.0 reshape_squeeze.39
  345.6 25.5 %all-to-all-done.3 = bf16[16,672,128]{2,1,0:T(8,128)(2,1)S(1)} async-done(((bf16[16,672,128]{2,1,0:T(8,128)(2,1)}), bf16[16,672,128]{2,1,0:T(8,128)(2,1)S(1)}, u32[]{:S(2)}, u32[]{:S(2)}) %all-to-all-start.3) | async-done | bytes 2752544 | tf_op jit(solution)/shard_map/all_to_all | solution.py:122
  372.3 2.4 select_convert_fusion
  374.7 5.2 %all-to-all-start.4 = ((bf16[16,672,128]{2,1,0:T(8,128)(2,1)}), bf16[16,672,128]{2,1,0:T(8,128)(2,1)}, u32[]{:S(2)}, u32[]{:S(2)}) async-start(bf16[16,672,128]{2,1,0:T(8,128)(2,1)} %select_convert_fusion), calls=%async_computation.4 | async-start | bytes 5505024 | tf_op jit(solution)/shard_map/all_to_all | solution.py:122
  379.9 4.4 fusion.70
  386.4 1.4 fusion.57
  387.7 3.5 fusion.6
  391.2 5.2 %copy.77 = f32[2,3584,128]{2,1,0:T(8,128)} copy(f32[2,3584,128]{1,2,0:T(8,128)} %fusion.6) | data formatting | bytes 7340032 | tf_op jit(solution)/shard_map/mul | solution.py:215
  396.4 3.2 convolution_multiply_fusion.2
  399.7 1.3 reshape.137
  401.0 13.0 %all-to-all-done.4 = bf16[16,672,128]{2,1,0:T(8,128)(2,1)} async-done(((bf16[16,672,128]{2,1,0:T(8,128)(2,1)}), bf16[16,672,128]{2,1,0:T(8,128)(2,1)}, u32[]{:S(2)}, u32[]{:S(2)}) %all-to-all-start.4) | async-done | bytes 2752544 | tf_op jit(solution)/shard_map/all_to_all | solution.py:122
  414.0 10.9 %fusion.16 = (bf16[16,672,128]{2,1,0:T(8,128)(2,1)}, bf16[16,672,128]{2,1,0:T(8,128)(2,1)S(1)}, bf16[16,672,128]{2,1,0:T(8,128)(2,1)}) fusion(bf16[16,224,128]{2,1,0:T(8,128)(2,1)} %reshape_squeeze.39, bf16[16,448,128]{2,1,0:T(8,128)(2,1)} %bitcast.199, bf16[16,672,128]{2,1,0:T(8,128)(2,1)} %all-to-all-done.4, f32[16,224,128]{2,1,0:T(8,128)} %reshape.137, ...), kind=kLoop, calls=%fused_computation.34 | loop fusion | flops 46792704 | bytes 24772608 | tf_op jit(solution)/shard_map/convert_element_type | solution.py:31
  424.9 37.9 %all_to_all.35 = bf16[16,672,128]{2,1,0:T(8,128)(2,1)S(1)} all-to-all(bf16[16,672,128]{2,1,0:T(8,128)(2,1)S(1)} %get-tuple-element.29), channel_id=1, replica_groups=mesh['expert'=16,'tensor'=8] {'expert'}, dimensions={0} | all-to-all | bytes 5505024 | tf_op jit(solution)/shard_map/all_to_all | solution.py:122
  462.9 1.8 broadcast_select_fusion
  464.7 4.9 all-to-all-start.6
  469.6 1.4 slice.116
  472.0 1.4 slice.118
  473.5 1.4 slice.120
  475.0 1.9 broadcast_in_dim_reshape.29
  476.9 1.9 broadcast_in_dim_reshape.31
  478.9 1.9 broadcast_in_dim_reshape.33
  480.8 22.9 %all-to-all-done.6 = bf16[16,672,128]{2,1,0:T(8,128)(2,1)} async-done(((bf16[16,672,128]{2,1,0:T(8,128)(2,1)}), bf16[16,672,128]{2,1,0:T(8,128)(2,1)}, u32[]{:S(2)}, u32[]{:S(2)}) %all-to-all-start.6) | async-done | bytes 2752544 | tf_op jit(solution)/shard_map/all_to_all | solution.py:122
  505.0 1.9 broadcast_in_dim_reshape.35
  506.9 2.9 slice.122
  (91 shorter events, 17.0 us)
Async XLA Ops:
  9.5 3.6 copy-start.5
  9.5 10.6 %copy-start.14 = (s32[256,4]{0,1:T(4,128)S(1)}, s32[256,4]{0,1:T(4,128)}, u32[]{:S(2)}) copy-start(s32[256,4]{0,1:T(4,128)} %param.12) | copy-start | bytes 12292
  13.1 17.0 %copy-start.15 = (f32[256,4]{0,1:T(4,128)S(1)}, f32[256,4]{0,1:T(4,128)}, u32[]{:S(2)}) copy-start(f32[256,4]{0,1:T(4,128)} %param.13) | copy-start | bytes 12292
  13.1 41.1 %all-to-all-start = ((bf16[16,672,128]{2,1,0:T(8,128)(2,1)}), bf16[16,672,128]{2,1,0:T(8,128)(2,1)}, u32[]{:S(2)}, u32[]{:S(2)}) async-start(bf16[16,672,128]{2,1,0:T(8,128)(2,1)} %pad_maximum_fusion.1), calls=%async_computation | async-start | bytes 5505024 | tf_op jit(solution)/shard_map/all_to_all | solution.py:122
  30.4 24.0 %copy-start.18 = (bf16[256,3584]{1,0:T(8,128)(2,1)S(1)}, bf16[256,3584]{1,0:T(8,128)(2,1)}, u32[]{:S(2)}) copy-start(bf16[256,3584]{1,0:T(8,128)(2,1)} %param.15) | copy-start | bytes 5505028
  73.2 5.7 %copy-start.16 = (s32[2]{0:T(128)S(1)}, s32[2]{0:T(128)}, u32[]{:S(2)}) copy-start(s32[2]{0:T(128)} %param.16) | copy-start | bytes 28
  73.2 150.8 %all-to-all-start.1 = ((bf16[16,2,40,3584]{3,2,1,0:T(8,128)(2,1)}), bf16[16,2,40,3584]{3,2,1,0:T(8,128)(2,1)}, u32[]{:S(2)}, u32[]{:S(2)}) async-start(bf16[16,2,40,3584]{3,2,1,0:T(8,128)(2,1)} %bitcast.181), calls=%async_computation.1 | async-start | bytes 18350080 | tf_op jit(solution)/shard_map/all_to_all | solution.py:122
  78.8 152.7 %all-gather.3.cloned.1.call-start = ((), (), s32[]{:S(2)}) async-start(), calls=%async_computation.7 | async-start | bytes 5849088 | tf_op jit(solution)/shard_map/all_gather | solution.py:183
  224.0 5.6 %copy-start.17 = (s32[16]{0:T(128)S(1)}, s32[16]{0:T(128)}, u32[]{:S(2)}) copy-start(s32[16]{0:T(128)} %param.17) | copy-start | bytes 196
  224.0 108.6 %all-to-all-start.2 = ((bf16[16,2,40,3584]{3,2,1,0:T(8,128)(2,1)}), bf16[16,2,40,3584]{3,2,1,0:T(8,128)(2,1)}, u32[]{:S(2)}, u32[]{:S(2)}) async-start(bf16[16,2,40,3584]{3,2,1,0:T(8,128)(2,1)} %bitcast.180), calls=%async_computation.2 | async-start | bytes 18350080 | tf_op jit(solution)/shard_map/all_to_all | solution.py:122
  233.5 1.7 copy-start.2
  237.1 4.4 slice-start
  241.5 2.1 copy-start.1
  241.6 2.1 copy-start.9
  242.9 2.1 copy-start.10
  245.0 5.8 %copy-start.11 = (f32[2,640,128]{2,1,0:T(8,128)S(1)}, f32[2,640,128]{2,1,0:T(8,128)}, u32[]{:S(2)}) copy-start(f32[2,640,128]{2,1,0:T(8,128)} %copy-done.10) | copy-start | bytes 1966084
  332.6 38.6 %all-to-all-start.3 = ((bf16[16,672,128]{2,1,0:T(8,128)(2,1)}), bf16[16,672,128]{2,1,0:T(8,128)(2,1)S(1)}, u32[]{:S(2)}, u32[]{:S(2)}) async-start(bf16[16,672,128]{2,1,0:T(8,128)(2,1)} %pad_maximum_fusion.3), calls=%async_computation.3 | async-start | bytes 5505024 | tf_op jit(solution)/shard_map/all_to_all | solution.py:122
  374.7 39.3 %all-to-all-start.4 = ((bf16[16,672,128]{2,1,0:T(8,128)(2,1)}), bf16[16,672,128]{2,1,0:T(8,128)(2,1)}, u32[]{:S(2)}, u32[]{:S(2)}) async-start(bf16[16,672,128]{2,1,0:T(8,128)(2,1)} %select_convert_fusion), calls=%async_computation.4 | async-start | bytes 5505024 | tf_op jit(solution)/shard_map/all_to_all | solution.py:122
  379.9 4.4 copy-start.6
  384.3 2.1 copy-start
  384.3 2.1 copy-start.8
  385.7 2.1 copy-start.12
  391.2 5.2 %copy-start.13 = (f32[2,640,128]{2,1,0:T(8,128)S(1)}, f32[2,640,128]{2,1,0:T(8,128)}, u32[]{:S(2)}) copy-start(f32[2,640,128]{2,1,0:T(8,128)} %copy-done.12) | copy-start | bytes 1966084
  464.7 39.0 %all-to-all-start.6 = ((bf16[16,672,128]{2,1,0:T(8,128)(2,1)}), bf16[16,672,128]{2,1,0:T(8,128)(2,1)}, u32[]{:S(2)}, u32[]{:S(2)}) async-start(bf16[16,672,128]{2,1,0:T(8,128)(2,1)} %broadcast_select_fusion), calls=%async_computation.6 | async-start | bytes 5505024 | tf_op jit(solution)/shard_map/all_to_all | solution.py:122
  469.6 2.4 copy-start.4
  471.0 2.5 copy-start.3
  473.4 1.6 copy-start.7
Sparse Core Ops, SparseCore 0:
  85.3 127.8 all-gather.2

commit v4 on v2

--- a/solution.py
+++ b/solution.py
@@ -74,7 +74,7 @@
     return row_index, row_scale
 
 
-def slot_terms(rows_token, rows_cotan, weight_in, weight_down, scale_in, scale_down):
+def slot_terms(rows_token, rows_cotan, weight_in, weight_down_t, scale_in, scale_down):
     joined = (
         jnp.einsum("rd,gdf->grf", rows_token, weight_in, preferred_element_type=jnp.float32)
         * scale_in
@@ -85,7 +85,7 @@
     active = gate_val * sigmoid_val
     hidden = (active * up_val).astype(jnp.bfloat16)
     back_grad = (
-        jnp.einsum("rd,fd->rf", rows_cotan, weight_down, preferred_element_type=jnp.float32)
+        jnp.einsum("rd,df->rf", rows_cotan, weight_down_t, preferred_element_type=jnp.float32)
         * scale_down
     )
     slope_gate = (back_grad * up_val * sigmoid_val * (1.0 + gate_val * (1.0 - sigmoid_val))).astype(
@@ -94,28 +94,37 @@
     slope_up = (back_grad * active).astype(jnp.bfloat16)
     slopes = jnp.stack([slope_gate, slope_up])
     grad_in = jnp.einsum("rd,grf->gdf", rows_token, slopes, preferred_element_type=jnp.float32)
-    grad_down = jnp.einsum("rf,rd->fd", hidden, rows_cotan, preferred_element_type=jnp.float32)
-    return (grad_in, grad_down)
+    grad_down_t = jnp.einsum("rf,rd->df", hidden, rows_cotan, preferred_element_type=jnp.float32)
+    return (grad_in, grad_down_t)
 
 
 def pack(part_in, part_down, groups):
+    return pack_t(part_in, part_down.T, groups)
+
+
+def pack_t(part_in, part_down_t, groups):
     width = part_in.shape[1]
     inner = part_in.shape[2]
     return jnp.concatenate(
         [
             part_in.reshape(groups, 2 * width // groups, inner),
-            part_down.reshape(groups, width // groups, inner),
+            part_down_t.reshape(groups, width // groups, inner),
         ],
         axis=1,
     )
 
 
-def unpack(packed, width, inner):
+def unpack_t(packed, width, inner):
     groups = packed.shape[0]
     split = 2 * width // groups
     part_in = packed[:, :split].reshape(2, width, inner)
-    part_down = packed[:, split:].reshape(inner, width)
-    return part_in, part_down
+    part_down_t = packed[:, split:].reshape(width, inner)
+    return part_in, part_down_t
+
+
+def unpack(packed, width, inner):
+    part_in, part_down_t = unpack_t(packed, width, inner)
+    return part_in, part_down_t.T
 
 
 def exchange(block):
@@ -182,8 +191,8 @@
 
     copy_rows = rows_of(1)
     copy_rows, held_packed = lax.optimization_barrier((copy_rows, held_packed))
-    held_in, held_down = unpack(held_packed, width, inner)
-    weight_sets = ((own_in, own_down), (held_in, held_down))
+    held_in, held_down_t = unpack_t(held_packed, width, inner)
+    weight_sets = ((own_in, own_down.T), (held_in, held_down_t))
 
     def terms_of(arrived_rows, add_which):
         return slot_terms(
@@ -197,7 +206,7 @@
 
     copy_in, copy_down = terms_of(copy_rows, 1)
     own_rows = rows_of(0)
-    copy_packed = pack(
+    copy_packed = pack_t(
         (copy_in * scale_in).astype(jnp.bfloat16),
         (copy_down * scale_down).astype(jnp.bfloat16),
         expert_count,
@@ -219,7 +228,7 @@
     ).astype(jnp.bfloat16)
     gathered = exchange(to_owner).astype(jnp.float32)
     is_hot = jnp.any(hot_experts == own_index)
-    own_grad = pack(grad_in, grad_down, expert_count)
+    own_grad = pack_t(grad_in, grad_down, expert_count)
     total = jnp.where(is_hot, own_grad.astype(jnp.bfloat16).astype(jnp.float32) + gathered, own_grad)
     stepped_p, averaged_p, squared_p = adam_step(
         own_packed,

time: 485 us -> 484 us (level)
  local copies, waits for them, and re-layouts: 66.8 us -> 61.7 us
    another operation x9 -> x2, local copies, waits for them, and re-layouts: 16.1 us -> 0.08 us  [the longest x3 8.27 us: pack(): part_down.reshape(groups, width // groups, inner)]
    unnamed x38 -> x45, local copies, waits for them, and re-layouts: 1.85 us -> 15.1 us
    reshape x3 -> x0, local copies, waits for them, and re-layouts: 5.37 us -> none  [the longest x2 3.42 us: pack(): part_down.reshape(groups, width // groups, inner)]
  transfers between devices with their start and end apart: 6 -> 6, of which waited for: 6 -> 6; matrix products, arithmetic and copies ran while one was open for 21% -> 20% of each run, Pallas kernels for 0% -> 0%
where the time goes in v4:
time: 484 us; the launch traced here: 483 us
  waiting for transfers between devices  168 us (35%)
  blocking collectives  146 us (30%)
  local copies, waits for them, and re-layouts  61.7 us (13%)
  other arithmetic  37.7 us (8%)
  matrix products  32.8 us (7%)
  starting transfers between devices  31.5 us (7%)
  between operations  4.99 us (1%)
    all_to_all x6, waiting for transfers between devices, exchange(): return lax.all_to_all(block, 'expert', 0, 0, tiled=True)  168 us
    all_to_all x2, blocking collectives, exchange(): return lax.all_to_all(block, 'expert', 0, 0, tiled=True)  146 us
    all_to_all x6, starting transfers between devices, exchange(): return lax.all_to_all(block, 'expert', 0, 0, tiled=True)  31.5 us
    unnamed x45, local copies, waits for them, and re-layouts  15.1 us
    dot_general x1, matrix products, gather_rows(): picked = jnp.dot(choose, source, preferred_element_type=jnp.float32)  12.3 us
    convert_element_type x1, other arithmetic, adam_step(): second_new.astype(jnp.bfloat16)  11 us
    slice x2, local copies, waits for them, and re-layouts, terms_of(): arrived_rows[:, 0].reshape(-1, width)  10.9 us
  transfers between devices with their start and end apart: 6, of which 6 were waited for; matrix products, arithmetic and copies ran while one was open for 20% of the time, Pallas kernels for 0%

profile of v4, /device:TPU:1, one launch (start us, length us, event | category | flops | bytes accessed | tf_op | source)
XLA Modules:
  0.0 483.2 jit_solution(13246549674154323382)
XLA Ops:
  0.6 1.6 copy.71
  2.2 3.6 pad_maximum_fusion.1
  5.8 7.0 %all-to-all-start = ((bf16[16,672,128]{2,1,0:T(8,128)(2,1)}), bf16[16,672,128]{2,1,0:T(8,128)(2,1)}, u32[]{:S(2)}, u32[]{:S(2)}) async-start(bf16[16,672,128]{2,1,0:T(8,128)(2,1)} %pad_maximum_fusion.1), calls=%async_computation | async-start | bytes 5505024 | tf_op jit(solution)/shard_map/all_to_all | solution.py:131
  16.5 9.0 %reduce-window.6 = s32[32,8,128]{2,1,0:T(8,128)S(1)} reduce-window(s32[32,8,128]{2,1,0:T(8,128)S(1)} %fusion.61, s32[]{:T(128)} %constant.29.clone.1), window={size=1x1x128 pad=0_0x0_0x127_0}, to_apply=%region_1.2 | reduce-window | flops 4161536 | bytes 262148 | tf_op jit(solution)/shard_map/reduce-window
  28.2 5.0 %gather_fusion = f32[1280]{0:T(1024)S(1)} fusion(f32[1024]{0:T(1024)S(1)} %reshape.154, s32[2048]{0:T(1024)S(1)} %pad_clamp_fusion), kind=kCustom, calls=%fused_computation | custom fusion | bytes 15360 | tf_op jit(solution)/shard_map/gather | solution.py:52
  34.8 1.3 broadcast_compare_fusion
  36.1 10.8 %all-to-all-done = bf16[16,672,128]{2,1,0:T(8,128)(2,1)} async-done(((bf16[16,672,128]{2,1,0:T(8,128)(2,1)}), bf16[16,672,128]{2,1,0:T(8,128)(2,1)}, u32[]{:S(2)}, u32[]{:S(2)}) %all-to-all-start) | async-done | bytes 2752544 | tf_op jit(solution)/shard_map/all_to_all | solution.py:131
  48.0 1.8 broadcast_select_fusion.1
  49.8 5.2 %all-to-all-start.2 = ((bf16[16,672,128]{2,1,0:T(8,128)(2,1)}), bf16[16,672,128]{2,1,0:T(8,128)(2,1)}, u32[]{:S(2)}, u32[]{:S(2)}) async-start(bf16[16,672,128]{2,1,0:T(8,128)(2,1)} %broadcast_select_fusion.1), calls=%async_computation.2 | async-start | bytes 5505024 | tf_op jit(solution)/shard_map/all_to_all | solution.py:131
  55.3 12.3 %multiply_convert_fusion = bf16[2560,3584]{1,0:T(8,128)(2,1)S(1)} fusion(f32[2560]{0:T(1024)S(1)} %mul.158, bf16[256,3584]{1,0:T(8,128)(2,1)S(1)} %copy-done.14, bf16[256,3584]{1,0:T(8,128)(2,1)} %param.14, s32[2560]{0:T(1024)S(1)} %eq.101), kind=kOutput, calls=%fused_computation.1 | convolution fusion | flops 9422241792 | bytes 22040576 | tf_op jit(solution)/shard_map/dot_general | solution.py:62
  67.5 6.5 %fusion.69 = (bf16[1280,3584]{1,0:T(8,128)(2,1)}, bf16[1280,3584]{1,0:T(8,128)(2,1)}) fusion(bf16[2560,3584]{1,0:T(8,128)(2,1)S(1)} %multiply_convert_fusion), kind=kLoop, calls=%fused_computation.128 | loop fusion | bytes 36700160 | tf_op jit(solution)/shard_map/slice | solution.py:190
  74.0 15.1 %all-to-all-done.2 = bf16[16,672,128]{2,1,0:T(8,128)(2,1)} async-done(((bf16[16,672,128]{2,1,0:T(8,128)(2,1)}), bf16[16,672,128]{2,1,0:T(8,128)(2,1)}, u32[]{:S(2)}, u32[]{:S(2)}) %all-to-all-start.2) | async-done | bytes 2752544 | tf_op jit(solution)/shard_map/all_to_all | solution.py:131
  89.1 108.3 %all_to_all.40 = bf16[16,2,40,3584]{3,2,1,0:T(8,128)(2,1)} all-to-all(bf16[16,2,40,3584]{3,2,1,0:T(8,128)(2,1)} %bitcast.217), channel_id=1, replica_groups=mesh['expert'=16,'tensor'=8] {'expert'}, dimensions={0} | all-to-all | bytes 18350080 | tf_op jit(solution)/shard_map/all_to_all | solution.py:131
  197.4 5.5 %all-to-all-start.3 = ((bf16[16,2,40,3584]{3,2,1,0:T(8,128)(2,1)}), bf16[16,2,40,3584]{3,2,1,0:T(8,128)(2,1)}, u32[]{:S(2)}, u32[]{:S(2)}) async-start(bf16[16,2,40,3584]{3,2,1,0:T(8,128)(2,1)} %bitcast.216), calls=%async_computation.3 | async-start | bytes 18350080 | tf_op jit(solution)/shard_map/all_to_all | solution.py:131
  202.9 1.6 slice.89
  204.5 2.2 slice.88
  206.7 4.3 fusion.71
  211.0 1.3 fusion.26
  213.1 1.4 fusion.56
  214.5 2.9 fusion.9
  217.4 2.9 copy.83
  220.3 3.7 fusion.10
  224.0 1.7 pad_maximum_fusion.3
  225.7 80.2 %all-to-all-done.3 = bf16[16,2,40,3584]{3,2,1,0:T(8,128)(2,1)} async-done(((bf16[16,2,40,3584]{3,2,1,0:T(8,128)(2,1)}), bf16[16,2,40,3584]{3,2,1,0:T(8,128)(2,1)}, u32[]{:S(2)}, u32[]{:S(2)}) %all-to-all-start.3) | async-done | bytes 9175072 | tf_op jit(solution)/shard_map/all_to_all | solution.py:131
  305.8 4.5 all-to-all-start.4
  310.3 2.2 copy.86
  312.5 2.2 copy.72
  314.7 1.3 iota_compare_fusion.4
  316.7 27.7 %all-to-all-done.4 = bf16[16,672,128]{2,1,0:T(8,128)(2,1)S(1)} async-done(((bf16[16,672,128]{2,1,0:T(8,128)(2,1)}), bf16[16,672,128]{2,1,0:T(8,128)(2,1)S(1)}, u32[]{:S(2)}, u32[]{:S(2)}) %all-to-all-start.4) | async-done | bytes 2752544 | tf_op jit(solution)/shard_map/all_to_all | solution.py:131
  345.6 2.4 select_convert_fusion
  347.9 4.5 all-to-all-start.5
  352.4 6.6 %fusion.70 = (bf16[16,1,40,3584]{3,2,1,0:T(8,128)(2,1)S(1)}, bf16[16,1,40,3584]{3,2,1,0:T(8,128)(2,1)}) fusion(bf16[16,2,40,3584]{3,2,1,0:T(8,128)(2,1)} %all-to-all-done.3), kind=kLoop, calls=%fused_computation.129 | loop fusion | bytes 18350080 | tf_op jit(solution)/shard_map/slice | solution.py:199
  359.1 1.3 fusion.23
  361.9 1.3 fusion.57
  363.2 3.5 fusion.6
  366.7 5.1 %copy.85 = f32[2,3584,128]{2,1,0:T(8,128)} copy(f32[2,3584,128]{1,2,0:T(8,128)} %fusion.6) | data formatting | bytes 7340032 | tf_op jit(solution)/shard_map/mul | solution.py:216
  371.8 5.1 %convolution_multiply_fusion.2 = f32[3584,128]{1,0:T(8,128)} fusion(bf16[640,3584]{1,0:T(8,128)(2,1)} %bitcast.230, f32[2,640,128]{2,1,0:T(8,128)} %copy-done.15), kind=kOutput, calls=%fused_computation.25 | convolution fusion | flops 588152832 | bytes 7077888 | tf_op jit(solution)/shard_map/rf,rd->df/dot_general | solution.py:97
  376.9 9.6 %all-to-all-done.5 = bf16[16,672,128]{2,1,0:T(8,128)(2,1)S(1)} async-done(((bf16[16,672,128]{2,1,0:T(8,128)(2,1)}), bf16[16,672,128]{2,1,0:T(8,128)(2,1)S(1)}, u32[]{:S(2)}, u32[]{:S(2)}) %all-to-all-start.5) | async-done | bytes 2752544 | tf_op jit(solution)/shard_map/all_to_all | solution.py:131
  386.5 1.5 copy-done
  388.0 11.0 %fusion.16 = (bf16[16,672,128]{2,1,0:T(8,128)(2,1)}, bf16[16,672,128]{2,1,0:T(8,128)(2,1)S(1)}, bf16[16,672,128]{2,1,0:T(8,128)(2,1)}) fusion(bf16[16,224,128]{2,1,0:T(8,128)(2,1)} %bitcast.236, bf16[16,448,128]{2,1,0:T(8,128)(2,1)} %bitcast.243, bf16[16,672,128]{2,1,0:T(8,128)(2,1)} %copy-done, f32[16,224,128]{2,1,0:T(8,128)} %bitcast.245, ...), kind=kLoop, calls=%fused_computation.34 | loop fusion | flops 46792704 | bytes 24772608 | tf_op jit(solution)/shard_map/convert_element_type | solution.py:31
  399.0 37.9 %all_to_all.41 = bf16[16,672,128]{2,1,0:T(8,128)(2,1)S(1)} all-to-all(bf16[16,672,128]{2,1,0:T(8,128)(2,1)S(1)} %get-tuple-element.53), channel_id=1, replica_groups=mesh['expert'=16,'tensor'=8] {'expert'}, dimensions={0} | all-to-all | bytes 5505024 | tf_op jit(solution)/shard_map/all_to_all | solution.py:131
  436.9 1.8 broadcast_select_fusion
  438.7 4.9 %all-to-all-start.7 = ((bf16[16,672,128]{2,1,0:T(8,128)(2,1)}), bf16[16,672,128]{2,1,0:T(8,128)(2,1)}, u32[]{:S(2)}, u32[]{:S(2)}) async-start(bf16[16,672,128]{2,1,0:T(8,128)(2,1)} %broadcast_select_fusion), calls=%async_computation.7 | async-start | bytes 5505024 | tf_op jit(solution)/shard_map/all_to_all | solution.py:131
  443.6 1.4 slice.116
  446.0 1.4 slice.118
  447.5 1.4 slice.120
  452.8 24.9 %all-to-all-done.7 = bf16[16,672,128]{2,1,0:T(8,128)(2,1)} async-done(((bf16[16,672,128]{2,1,0:T(8,128)(2,1)}), bf16[16,672,128]{2,1,0:T(8,128)(2,1)}, u32[]{:S(2)}, u32[]{:S(2)}) %all-to-all-start.7) | async-done | bytes 2752544 | tf_op jit(solution)/shard_map/all_to_all | solution.py:131
  480.3 2.9 slice.122
  (81 shorter events, 16.7 us)
Async XLA Ops:
  2.2 3.6 copy-start.3
  2.2 10.7 %copy-start.12 = (s32[2]{0:T(128)S(1)}, s32[2]{0:T(128)}, u32[]{:S(2)}) copy-start(s32[2]{0:T(128)} %param.16) | copy-start | bytes 28
  2.2 11.2 %copy-start.10 = (s32[256,4]{0,1:T(4,128)S(1)}, s32[256,4]{0,1:T(4,128)}, u32[]{:S(2)}) copy-start(s32[256,4]{0,1:T(4,128)} %param.12) | copy-start | bytes 12292
  5.8 20.2 %copy-start.11 = (f32[256,4]{0,1:T(4,128)S(1)}, f32[256,4]{0,1:T(4,128)}, u32[]{:S(2)}) copy-start(f32[256,4]{0,1:T(4,128)} %param.13) | copy-start | bytes 12292
  5.8 41.1 %all-to-all-start = ((bf16[16,672,128]{2,1,0:T(8,128)(2,1)}), bf16[16,672,128]{2,1,0:T(8,128)(2,1)}, u32[]{:S(2)}, u32[]{:S(2)}) async-start(bf16[16,672,128]{2,1,0:T(8,128)(2,1)} %pad_maximum_fusion.1), calls=%async_computation | async-start | bytes 5505024 | tf_op jit(solution)/shard_map/all_to_all | solution.py:131
  26.3 8.5 %copy-start.13 = (s32[16]{0:T(128)S(1)}, s32[16]{0:T(128)}, u32[]{:S(2)}) copy-start(s32[16]{0:T(128)} %param.17) | copy-start | bytes 196
  36.1 19.1 %copy-start.14 = (bf16[256,3584]{1,0:T(8,128)(2,1)S(1)}, bf16[256,3584]{1,0:T(8,128)(2,1)}, u32[]{:S(2)}) copy-start(bf16[256,3584]{1,0:T(8,128)(2,1)} %param.15) | copy-start | bytes 5505028
  49.8 39.4 %all-to-all-start.2 = ((bf16[16,672,128]{2,1,0:T(8,128)(2,1)}), bf16[16,672,128]{2,1,0:T(8,128)(2,1)}, u32[]{:S(2)}, u32[]{:S(2)}) async-start(bf16[16,672,128]{2,1,0:T(8,128)(2,1)} %broadcast_select_fusion.1), calls=%async_computation.2 | async-start | bytes 5505024 | tf_op jit(solution)/shard_map/all_to_all | solution.py:131
  197.4 108.4 %all-to-all-start.3 = ((bf16[16,2,40,3584]{3,2,1,0:T(8,128)(2,1)}), bf16[16,2,40,3584]{3,2,1,0:T(8,128)(2,1)}, u32[]{:S(2)}, u32[]{:S(2)}) async-start(bf16[16,2,40,3584]{3,2,1,0:T(8,128)(2,1)} %bitcast.216), calls=%async_computation.3 | async-start | bytes 18350080 | tf_op jit(solution)/shard_map/all_to_all | solution.py:131
  211.0 2.2 copy-start.5
  211.0 2.1 copy-start.9
  212.3 2.1 copy-start.16
  214.5 5.8 %copy-start.17 = (f32[2,640,128]{2,1,0:T(8,128)S(1)}, f32[2,640,128]{2,1,0:T(8,128)}, u32[]{:S(2)}) copy-start(f32[2,640,128]{2,1,0:T(8,128)} %copy-done.16) | copy-start | bytes 1966084
  305.8 38.6 %all-to-all-start.4 = ((bf16[16,672,128]{2,1,0:T(8,128)(2,1)}), bf16[16,672,128]{2,1,0:T(8,128)(2,1)S(1)}, u32[]{:S(2)}, u32[]{:S(2)}) async-start(bf16[16,672,128]{2,1,0:T(8,128)(2,1)} %pad_maximum_fusion.3), calls=%async_computation.4 | async-start | bytes 5505024 | tf_op jit(solution)/shard_map/all_to_all | solution.py:131
  347.9 38.6 %all-to-all-start.5 = ((bf16[16,672,128]{2,1,0:T(8,128)(2,1)}), bf16[16,672,128]{2,1,0:T(8,128)(2,1)S(1)}, u32[]{:S(2)}, u32[]{:S(2)}) async-start(bf16[16,672,128]{2,1,0:T(8,128)(2,1)} %select_convert_fusion), calls=%async_computation.5 | async-start | bytes 5505024 | tf_op jit(solution)/shard_map/all_to_all | solution.py:131
  352.4 6.7 %copy-start.4 = (bf16[1,2,3584,128]{3,2,1,0:T(8,128)(2,1)S(1)}, bf16[1,2,3584,128]{3,2,1,0:T(8,128)(2,1)}, u32[]{:S(2)}) copy-start(bf16[1,2,3584,128]{3,2,1,0:T(8,128)(2,1)} %param.18) | copy-start | bytes 5505028
  359.1 2.3 copy-start.6
  359.1 2.8 copy-start.8
  360.4 2.8 copy-start.15
  386.5 1.5 copy-start
  438.7 39.0 %all-to-all-start.7 = ((bf16[16,672,128]{2,1,0:T(8,128)(2,1)}), bf16[16,672,128]{2,1,0:T(8,128)(2,1)}, u32[]{:S(2)}, u32[]{:S(2)}) async-start(bf16[16,672,128]{2,1,0:T(8,128)(2,1)} %broadcast_select_fusion), calls=%async_computation.7 | async-start | bytes 5505024 | tf_op jit(solution)/shard_map/all_to_all | solution.py:131
  443.6 2.4 copy-start.2
  445.0 2.5 copy-start.1
  447.5 1.6 copy-start.7

commit v5 on v4

--- a/solution.py
+++ b/solution.py
@@ -226,16 +226,28 @@
         sums[0][None],
         jnp.where((sources == hot_experts[1])[:, None, None], sums[1][None], 0.0),
     ).astype(jnp.bfloat16)
-    gathered = exchange(to_owner).astype(jnp.float32)
+    gathered_low = exchange(to_owner)
     is_hot = jnp.any(hot_experts == own_index)
-    own_grad = pack_t(grad_in, grad_down, expert_count)
-    total = jnp.where(is_hot, own_grad.astype(jnp.bfloat16).astype(jnp.float32) + gathered, own_grad)
-    stepped_p, averaged_p, squared_p = adam_step(
-        own_packed,
-        pack(mean_in[0], mean_down[0], expert_count),
-        pack(square_in[0], square_down[0], expert_count),
-        total,
-    )
+
+    def adam_of(gathered_low, grad_in, grad_down):
+        own_grad = pack_t(grad_in, grad_down, expert_count)
+        total = jnp.where(
+            is_hot,
+            own_grad.astype(jnp.bfloat16).astype(jnp.float32) + gathered_low.astype(jnp.float32),
+            own_grad,
+        )
+        return adam_step(
+            own_packed,
+            pack(mean_in[0], mean_down[0], expert_count),
+            pack(square_in[0], square_down[0], expert_count),
+            total,
+        )
+
+    stepped_p = adam_of(gathered_low, grad_in, grad_down)[0]
+    stepped_p, gathered_low, grad_in, grad_down = lax.optimization_barrier(
+        (stepped_p, gathered_low, grad_in, grad_down)
+    )
+    _, averaged_p, squared_p = adam_of(gathered_low, grad_in, grad_down)
     copied_in, copied_down = unpack(spread_hot(stepped_p, hot_experts, replica_of), width, inner)
     stepped_in, stepped_down = unpack(stepped_p, width, inner)
     averaged_in, averaged_down = unpack(averaged_p, width, inner)

time: 484 us -> 483 us (level)
  waiting for transfers between devices: 168 us -> 158 us
    all_to_all x6, waiting for transfers between devices: 168 us -> 158 us  [exchange(): return lax.all_to_all(block, 'expert', 0, 0, tiled=True)]
    convert_element_type x0 -> x1, other arithmetic: none -> 9.03 us  [adam_step(): weight_new.astype(jnp.bfloat16)]
    optimization_barrier x0 -> x1, local copies, waits for them, and re-layouts: none -> 5.29 us  [body(): lax.optimization_barrier((stepped_p, gathered_low, grad_in, grad_down))]
    convert_element_type x1, other arithmetic: 11 us -> 6.08 us  [adam_step(): second_new.astype(jnp.bfloat16)]
    unnamed x45 -> x43, local copies, waits for them, and re-layouts: 15.1 us -> 15.2 us
  transfers between devices with their start and end apart: 6 -> 6, of which waited for: 6 -> 6; matrix products, arithmetic and copies ran while one was open for 20% -> 23% of each run, Pallas kernels for 0% -> 0%
where the time goes in v5:
time: 483 us; the launch traced here: 482 us
  waiting for transfers between devices  158 us (33%)
  blocking collectives  146 us (30%)
  local copies, waits for them, and re-layouts  66.2 us (14%)
  other arithmetic  41.8 us (9%)
  matrix products  32.8 us (7%)
  starting transfers between devices  31.5 us (7%)
  between operations  5 us (1%)
    all_to_all x6, waiting for transfers between devices, exchange(): return lax.all_to_all(block, 'expert', 0, 0, tiled=True)  158 us
    all_to_all x2, blocking collectives, exchange(): return lax.all_to_all(block, 'expert', 0, 0, tiled=True)  146 us
    all_to_all x6, starting transfers between devices, exchange(): return lax.all_to_all(block, 'expert', 0, 0, tiled=True)  31.5 us
    unnamed x43, local copies, waits for them, and re-layouts  15.2 us
    dot_general x1, matrix products, gather_rows(): picked = jnp.dot(choose, source, preferred_element_type=jnp.float32)  12.3 us
    slice x2, local copies, waits for them, and re-layouts, terms_of(): arrived_rows[:, 0].reshape(-1, width)  10.9 us
  transfers between devices with their start and end apart: 6, of which 6 were waited for; matrix products, arithmetic and copies ran while one was open for 23% of the time, Pallas kernels for 0%

profile of v5, /device:TPU:1, one launch (start us, length us, event | category | flops | bytes accessed | tf_op | source)
XLA Modules:
  0.0 481.7 jit_solution(14164731610658592177)
XLA Ops:
  0.6 1.6 copy.74
  2.2 3.6 pad_maximum_fusion.2
  5.8 7.0 %all-to-all-start = ((bf16[16,672,128]{2,1,0:T(8,128)(2,1)}), bf16[16,672,128]{2,1,0:T(8,128)(2,1)}, u32[]{:S(2)}, u32[]{:S(2)}) async-start(bf16[16,672,128]{2,1,0:T(8,128)(2,1)} %pad_maximum_fusion.2), calls=%async_computation | async-start | bytes 5505024 | tf_op jit(solution)/shard_map/all_to_all | solution.py:131
  16.5 9.0 %reduce-window.6 = s32[32,8,128]{2,1,0:T(8,128)S(1)} reduce-window(s32[32,8,128]{2,1,0:T(8,128)S(1)} %fusion.65, s32[]{:T(128)} %constant.29.clone.1), window={size=1x1x128 pad=0_0x0_0x127_0}, to_apply=%region_1.2 | reduce-window | flops 4161536 | bytes 262148 | tf_op jit(solution)/shard_map/reduce-window
  28.2 5.0 %gather_fusion = f32[1280]{0:T(1024)S(1)} fusion(f32[1024]{0:T(1024)S(1)} %reshape.162, s32[2048]{0:T(1024)S(1)} %pad_clamp_fusion), kind=kCustom, calls=%fused_computation | custom fusion | bytes 15360 | tf_op jit(solution)/shard_map/gather | solution.py:52
  36.1 10.8 %all-to-all-done = bf16[16,672,128]{2,1,0:T(8,128)(2,1)} async-done(((bf16[16,672,128]{2,1,0:T(8,128)(2,1)}), bf16[16,672,128]{2,1,0:T(8,128)(2,1)}, u32[]{:S(2)}, u32[]{:S(2)}) %all-to-all-start) | async-done | bytes 2752544 | tf_op jit(solution)/shard_map/all_to_all | solution.py:131
  48.4 1.8 broadcast_select_fusion.1
  50.2 5.2 %all-to-all-start.2 = ((bf16[16,672,128]{2,1,0:T(8,128)(2,1)}), bf16[16,672,128]{2,1,0:T(8,128)(2,1)}, u32[]{:S(2)}, u32[]{:S(2)}) async-start(bf16[16,672,128]{2,1,0:T(8,128)(2,1)} %broadcast_select_fusion.1), calls=%async_computation.2 | async-start | bytes 5505024 | tf_op jit(solution)/shard_map/all_to_all | solution.py:131
  55.4 12.3 %multiply_convert_fusion = bf16[2560,3584]{1,0:T(8,128)(2,1)S(1)} fusion(f32[2560]{0:T(1024)S(1)} %mul.159, bf16[256,3584]{1,0:T(8,128)(2,1)S(1)} %copy-done.13, bf16[256,3584]{1,0:T(8,128)(2,1)} %param.14, s32[2560]{0:T(1024)S(1)} %eq.101), kind=kOutput, calls=%fused_computation.1 | convolution fusion | flops 9422241792 | bytes 22040576 | tf_op jit(solution)/shard_map/dot_general | solution.py:62
  67.7 6.5 %fusion.73 = (bf16[1280,3584]{1,0:T(8,128)(2,1)}, bf16[1280,3584]{1,0:T(8,128)(2,1)}) fusion(bf16[2560,3584]{1,0:T(8,128)(2,1)S(1)} %multiply_convert_fusion), kind=kLoop, calls=%fused_computation.136 | loop fusion | bytes 36700160 | tf_op jit(solution)/shard_map/slice | solution.py:190
  74.2 15.4 %all-to-all-done.2 = bf16[16,672,128]{2,1,0:T(8,128)(2,1)} async-done(((bf16[16,672,128]{2,1,0:T(8,128)(2,1)}), bf16[16,672,128]{2,1,0:T(8,128)(2,1)}, u32[]{:S(2)}, u32[]{:S(2)}) %all-to-all-start.2) | async-done | bytes 2752544 | tf_op jit(solution)/shard_map/all_to_all | solution.py:131
  89.5 108.2 %all_to_all.40 = bf16[16,2,40,3584]{3,2,1,0:T(8,128)(2,1)} all-to-all(bf16[16,2,40,3584]{3,2,1,0:T(8,128)(2,1)} %bitcast.219), channel_id=1, replica_groups=mesh['expert'=16,'tensor'=8] {'expert'}, dimensions={0} | all-to-all | bytes 18350080 | tf_op jit(solution)/shard_map/all_to_all | solution.py:131
  197.8 5.5 %all-to-all-start.3 = ((bf16[16,2,40,3584]{3,2,1,0:T(8,128)(2,1)}), bf16[16,2,40,3584]{3,2,1,0:T(8,128)(2,1)}, u32[]{:S(2)}, u32[]{:S(2)}) async-start(bf16[16,2,40,3584]{3,2,1,0:T(8,128)(2,1)} %bitcast.218), calls=%async_computation.3 | async-start | bytes 18350080 | tf_op jit(solution)/shard_map/all_to_all | solution.py:131
  203.3 1.6 slice.89
  204.9 2.2 slice.88
  207.1 4.3 fusion.75
  211.4 1.3 fusion.30
  213.5 1.4 fusion.60
  214.9 2.9 fusion.14
  217.8 2.9 copy.86
  220.7 3.7 fusion.15
  224.4 1.7 pad_maximum_fusion.4
  226.1 80.2 %all-to-all-done.3 = bf16[16,2,40,3584]{3,2,1,0:T(8,128)(2,1)} async-done(((bf16[16,2,40,3584]{3,2,1,0:T(8,128)(2,1)}), bf16[16,2,40,3584]{3,2,1,0:T(8,128)(2,1)}, u32[]{:S(2)}, u32[]{:S(2)}) %all-to-all-start.3) | async-done | bytes 9175072 | tf_op jit(solution)/shard_map/all_to_all | solution.py:131
  306.2 4.5 all-to-all-start.4
  310.7 2.2 copy.89
  312.9 2.2 copy.75
  317.1 27.7 %all-to-all-done.4 = bf16[16,672,128]{2,1,0:T(8,128)(2,1)S(1)} async-done(((bf16[16,672,128]{2,1,0:T(8,128)(2,1)}), bf16[16,672,128]{2,1,0:T(8,128)(2,1)S(1)}, u32[]{:S(2)}, u32[]{:S(2)}) %all-to-all-start.4) | async-done | bytes 2752544 | tf_op jit(solution)/shard_map/all_to_all | solution.py:131
  346.0 2.4 select_convert_fusion
  348.3 4.5 all-to-all-start.5
  352.8 6.6 %fusion.74 = (bf16[16,1,40,3584]{3,2,1,0:T(8,128)(2,1)S(1)}, bf16[16,1,40,3584]{3,2,1,0:T(8,128)(2,1)}) fusion(bf16[16,2,40,3584]{3,2,1,0:T(8,128)(2,1)} %all-to-all-done.3), kind=kLoop, calls=%fused_computation.137 | loop fusion | bytes 18350080 | tf_op jit(solution)/shard_map/slice | solution.py:199
  359.5 1.3 fusion.27
  362.3 1.3 fusion.61
  363.6 3.4 fusion.11
  367.1 5.1 %copy.88 = f32[2,3584,128]{2,1,0:T(8,128)} copy(f32[2,3584,128]{1,2,0:T(8,128)} %fusion.11) | data formatting | bytes 7340032 | tf_op jit(solution)/shard_map/mul | solution.py:216
  372.2 5.1 %convolution_multiply_fusion.2 = f32[3584,128]{1,0:T(8,128)} fusion(bf16[640,3584]{1,0:T(8,128)(2,1)} %bitcast.244, f32[2,640,128]{2,1,0:T(8,128)} %copy-done.14), kind=kOutput, calls=%fused_computation.34 | convolution fusion | flops 588152832 | bytes 7077888 | tf_op jit(solution)/shard_map/rf,rd->df/dot_general | solution.py:97
  377.3 9.6 %all-to-all-done.5 = bf16[16,672,128]{2,1,0:T(8,128)(2,1)S(1)} async-done(((bf16[16,672,128]{2,1,0:T(8,128)(2,1)}), bf16[16,672,128]{2,1,0:T(8,128)(2,1)S(1)}, u32[]{:S(2)}, u32[]{:S(2)}) %all-to-all-start.5) | async-done | bytes 2752544 | tf_op jit(solution)/shard_map/all_to_all | solution.py:131
  386.9 1.6 copy-done.1
  388.4 9.0 %fusion.2 = bf16[16,672,128]{2,1,0:T(8,128)(2,1)S(1)} fusion(bf16[16,672,128]{2,1,0:T(8,128)(2,1)} %copy-done.1, f32[16,224,128]{2,1,0:T(8,128)} %bitcast.240, f32[16,448,128]{2,1,0:T(8,128)} %bitcast.225, pred[]{:T(512)} %compare_reduce_fusion.1, bf16[16,224,128]{2,1,0:T(8,128)(2,1)} %bitcast.229, bf16[16,448,128]{2,1,0:T(8,128)(2,1)} %bitcast.236, ...), kind=kLoop, calls=%fused_computation.14 | loop fusion | flops 44040192 | bytes 19267584 | tf_op jit(solution)/shard_map/convert_element_type | solution.py:29
  397.5 37.9 %all_to_all.41 = bf16[16,672,128]{2,1,0:T(8,128)(2,1)S(1)} all-to-all(bf16[16,672,128]{2,1,0:T(8,128)(2,1)S(1)} %fusion.2), channel_id=1, replica_groups=mesh['expert'=16,'tensor'=8] {'expert'}, dimensions={0} | all-to-all | bytes 5505024 | tf_op jit(solution)/shard_map/all_to_all | solution.py:131
  435.4 1.8 broadcast_select_fusion
  437.3 4.8 %all-to-all-start.7 = ((bf16[16,672,128]{2,1,0:T(8,128)(2,1)}), bf16[16,672,128]{2,1,0:T(8,128)(2,1)}, u32[]{:S(2)}, u32[]{:S(2)}) async-start(bf16[16,672,128]{2,1,0:T(8,128)(2,1)} %broadcast_select_fusion), calls=%async_computation.7 | async-start | bytes 5505024 | tf_op jit(solution)/shard_map/all_to_all | solution.py:131
  442.1 1.4 slice.98
  443.6 5.3 %copy.90 = f32[2,3584,128]{2,1,0:T(8,128)} copy(f32[2,3584,128]{1,2,0:T(8,128)} %fusion.11) | data formatting | bytes 7340032 | tf_op jit(solution)/shard_map/optimization_barrier | solution.py:247
  448.9 6.1 %fusion.10 = (bf16[16,672,128]{2,1,0:T(8,128)(2,1)S(1)}, bf16[16,672,128]{2,1,0:T(8,128)(2,1)S(1)}) fusion(bf16[16,224,128]{2,1,0:T(8,128)(2,1)} %bitcast.230, bf16[16,448,128]{2,1,0:T(8,128)(2,1)} %bitcast.237, bf16[16,672,128]{2,1,0:T(8,128)(2,1)S(1)} %copy-done.2, f32[16,224,128]{2,1,0:T(8,128)} %bitcast.241, f32[16,448,128]{2,1,0:T(8,128)} %bitcast.226, ...), kind=kLoop, calls=%fused_computation.22 | loop fusion | flops 31653888 | bytes 19267584 | tf_op jit(solution)/shard_map/convert_element_type | solution.py:31
  454.9 1.4 slice.116
  456.4 1.4 slice.118
  461.7 14.6 %all-to-all-done.7 = bf16[16,672,128]{2,1,0:T(8,128)(2,1)} async-done(((bf16[16,672,128]{2,1,0:T(8,128)(2,1)}), bf16[16,672,128]{2,1,0:T(8,128)(2,1)}, u32[]{:S(2)}, u32[]{:S(2)}) %all-to-all-start.7) | async-done | bytes 2752544 | tf_op jit(solution)/shard_map/all_to_all | solution.py:131
  478.8 2.9 slice.120
  (82 shorter events, 18.4 us)
Async XLA Ops:
  2.2 3.6 copy-start.3
  2.2 10.7 %copy-start.11 = (s32[2]{0:T(128)S(1)}, s32[2]{0:T(128)}, u32[]{:S(2)}) copy-start(s32[2]{0:T(128)} %param.16) | copy-start | bytes 28
  2.2 11.2 %copy-start.9 = (s32[256,4]{0,1:T(4,128)S(1)}, s32[256,4]{0,1:T(4,128)}, u32[]{:S(2)}) copy-start(s32[256,4]{0,1:T(4,128)} %param.12) | copy-start | bytes 12292
  5.8 21.2 %copy-start.10 = (f32[256,4]{0,1:T(4,128)S(1)}, f32[256,4]{0,1:T(4,128)}, u32[]{:S(2)}) copy-start(f32[256,4]{0,1:T(4,128)} %param.13) | copy-start | bytes 12292
  5.8 41.1 %all-to-all-start = ((bf16[16,672,128]{2,1,0:T(8,128)(2,1)}), bf16[16,672,128]{2,1,0:T(8,128)(2,1)}, u32[]{:S(2)}, u32[]{:S(2)}) async-start(bf16[16,672,128]{2,1,0:T(8,128)(2,1)} %pad_maximum_fusion.2), calls=%async_computation | async-start | bytes 5505024 | tf_op jit(solution)/shard_map/all_to_all | solution.py:131
  26.1 8.7 %copy-start.12 = (s32[16]{0:T(128)S(1)}, s32[16]{0:T(128)}, u32[]{:S(2)}) copy-start(s32[16]{0:T(128)} %param.17) | copy-start | bytes 196
  47.2 8.2 %copy-start.13 = (bf16[256,3584]{1,0:T(8,128)(2,1)S(1)}, bf16[256,3584]{1,0:T(8,128)(2,1)}, u32[]{:S(2)}) copy-start(bf16[256,3584]{1,0:T(8,128)(2,1)} %param.15) | copy-start | bytes 5505028
  50.2 39.4 %all-to-all-start.2 = ((bf16[16,672,128]{2,1,0:T(8,128)(2,1)}), bf16[16,672,128]{2,1,0:T(8,128)(2,1)}, u32[]{:S(2)}, u32[]{:S(2)}) async-start(bf16[16,672,128]{2,1,0:T(8,128)(2,1)} %broadcast_select_fusion.1), calls=%async_computation.2 | async-start | bytes 5505024 | tf_op jit(solution)/shard_map/all_to_all | solution.py:131
  197.8 108.4 %all-to-all-start.3 = ((bf16[16,2,40,3584]{3,2,1,0:T(8,128)(2,1)}), bf16[16,2,40,3584]{3,2,1,0:T(8,128)(2,1)}, u32[]{:S(2)}, u32[]{:S(2)}) async-start(bf16[16,2,40,3584]{3,2,1,0:T(8,128)(2,1)} %bitcast.218), calls=%async_computation.3 | async-start | bytes 18350080 | tf_op jit(solution)/shard_map/all_to_all | solution.py:131
  211.4 2.2 copy-start.5
  211.4 2.1 copy-start.8
  212.7 2.1 copy-start.15
  214.9 5.8 %copy-start.16 = (f32[2,640,128]{2,1,0:T(8,128)S(1)}, f32[2,640,128]{2,1,0:T(8,128)}, u32[]{:S(2)}) copy-start(f32[2,640,128]{2,1,0:T(8,128)} %copy-done.15) | copy-start | bytes 1966084
  306.2 38.6 %all-to-all-start.4 = ((bf16[16,672,128]{2,1,0:T(8,128)(2,1)}), bf16[16,672,128]{2,1,0:T(8,128)(2,1)S(1)}, u32[]{:S(2)}, u32[]{:S(2)}) async-start(bf16[16,672,128]{2,1,0:T(8,128)(2,1)} %pad_maximum_fusion.4), calls=%async_computation.4 | async-start | bytes 5505024 | tf_op jit(solution)/shard_map/all_to_all | solution.py:131
  348.3 38.6 %all-to-all-start.5 = ((bf16[16,672,128]{2,1,0:T(8,128)(2,1)}), bf16[16,672,128]{2,1,0:T(8,128)(2,1)S(1)}, u32[]{:S(2)}, u32[]{:S(2)}) async-start(bf16[16,672,128]{2,1,0:T(8,128)(2,1)} %select_convert_fusion), calls=%async_computation.5 | async-start | bytes 5505024 | tf_op jit(solution)/shard_map/all_to_all | solution.py:131
  352.8 6.6 %copy-start.4 = (bf16[1,2,3584,128]{3,2,1,0:T(8,128)(2,1)S(1)}, bf16[1,2,3584,128]{3,2,1,0:T(8,128)(2,1)}, u32[]{:S(2)}) copy-start(bf16[1,2,3584,128]{3,2,1,0:T(8,128)(2,1)} %param.18) | copy-start | bytes 5505028
  359.5 2.3 copy-start.6
  359.5 2.8 copy-start.7
  360.8 2.8 copy-start.14
  386.9 1.6 copy-start.1
  397.5 46.1 %copy-start = (bf16[16,672,128]{2,1,0:T(8,128)(2,1)}, bf16[16,672,128]{2,1,0:T(8,128)(2,1)S(1)}, u32[]{:S(2)}) copy-start(bf16[16,672,128]{2,1,0:T(8,128)(2,1)S(1)} %fusion.2) | copy-start | bytes 8257540
  437.3 39.0 %all-to-all-start.7 = ((bf16[16,672,128]{2,1,0:T(8,128)(2,1)}), bf16[16,672,128]{2,1,0:T(8,128)(2,1)}, u32[]{:S(2)}, u32[]{:S(2)}) async-start(bf16[16,672,128]{2,1,0:T(8,128)(2,1)} %broadcast_select_fusion), calls=%async_computation.7 | async-start | bytes 5505024 | tf_op jit(solution)/shard_map/all_to_all | solution.py:131
  443.6 5.3 %copy-start.2 = (bf16[16,672,128]{2,1,0:T(8,128)(2,1)S(1)}, bf16[16,672,128]{2,1,0:T(8,128)(2,1)}, u32[]{:S(2)}) copy-start(bf16[16,672,128]{2,1,0:T(8,128)(2,1)} %copy-done.1) | copy-start | bytes 8257540
  456.3 1.5 slice-start
